TPU v7x, 128 devices: a whole 4x4x4 slice. The times are simulated.
128 devices in a mesh: view: 4 (over y), gauss: 32 (over z, x, core).
Axes of the slice: x: 4, y: 4, z: 4, core: 2. Of those that a mesh axis runs over, the one named last changes fastest.
Arguments:
- jac: bfloat16 [4, 128, 59, 128, 256], P('view', 'gauss'), may hold values from -0.375 to 0.375
- tile_count: int32 [4, 32], P('view', 'gauss'), may hold values from 1 to 4, as said below
- tile_block: int32 [4, 128], P('view', 'gauss'), may hold values from 0 to 1
- tile_pix: int32 [4, 128], P('view', 'gauss'), may hold values from 0 to 4095
- residual: bfloat16 [4, 4096, 256], P('view'), may hold values from -6 to 6
- direction: bfloat16 [64, 59, 128], P('gauss'), may hold values from -0.75 to 0.75
Outputs:
- gradient: float32 [64, 59, 128], P('gauss')
- curvature: float32 [64, 59, 128], P('gauss')
- precond: float32 [64, 59, 59, 128], P('gauss')
Inputs may be any that keep to these rules, and one draw needn't show every extreme that they name: `tile_count`: every device has at least one live tile, and some device has all 4 slots live.
All inputs are finite; a program needn't handle non-finite values.
Results may differ from a plain program's by a relative error of at most 0.0028.
Values sent between devices are 32-bit elements; how exact they have to be, the bound alone decides.
No kernel may reach another device: no remote copies, remote signals or barrier semaphores. Data moves between devices by JAX's collectives and lax.ppermute only.
A program may use at most 128 MiB of HBM per device.

v0:
```python
import math

import jax
import jax.numpy as jnp
import numpy as np
from jax import lax
from jax.sharding import PartitionSpec as P
from jax.experimental import pallas as pl
from jax.experimental.pallas import tpu as pltpu


def side_by_side(arrays, axis, dim, along):
    widths = [math.prod(a.shape[along:]) for a in arrays]
    both = jnp.concatenate(
        [a.reshape(*a.shape[:along], w) for a, w in zip(arrays, widths)], axis=along
    )
    result = lax.all_gather(both, axis, axis=dim, tiled=True)
    blocks = jnp.split(result, [sum(widths[:k]) for k in range(1, len(widths))], axis=along)
    return tuple(
        (b.reshape(*result.shape[:along], *a.shape[along:]) for a, b in zip(arrays, blocks))
    )


def copy_for_each(array, axis):
    length = lax.axis_size(axis)
    return lax.all_to_all(
        jnp.broadcast_to(array[None], (length, *array.shape)), axis, 0, 0, tiled=True
    )


def over_copies(array, axis):
    everything = copy_for_each(array, axis)
    return jnp.sum(everything, axis=0)


P_PAD = 64
GROUP = 4


def row_offsets(size):
    return [p * size - p * (p - 1) // 2 for p in range(size)]


def gram_kernel(w_ref, jac_ref, out_ref, xf_ref, sc_ref, acc_ref):
    t = pl.program_id(0)
    size = jac_ref.shape[0]
    gb = jac_ref.shape[1]
    nb = acc_ref.shape[0]

    @pl.when(t == 0)
    def _init():
        for h in range(xf_ref.shape[0]):
            xf_ref[h, pl.ds(size * gb, (P_PAD - size) * gb), :] = jnp.zeros(((P_PAD - size) * gb, 128), jnp.float32)
        acc_ref[...] = jnp.zeros(acc_ref.shape, jnp.float32)

    halves = xf_ref.shape[0]
    for p in range(size):
        for h in range(halves):
            xf_ref[h, pl.ds(p * gb, gb), :] = jac_ref[p, :, h * 128:(h + 1) * 128].astype(jnp.float32)

    for c in range(gb // GROUP):
        parts = [
            jnp.concatenate([xf_ref[h, pl.ds(c * GROUP + i, P_PAD, stride=gb), :] for h in range(halves)], axis=1)
            for i in range(GROUP)
        ]
        a = jnp.concatenate(parts, axis=0).astype(jnp.bfloat16)
        prod = lax.dot_general(a, a, (((1,), (1,)), ((), ())), preferred_element_type=jnp.float32)
        for i in range(GROUP):
            g = c * GROUP + i
            lane0 = 128 * ((i * P_PAD) // 128)
            sc_ref[pl.ds(g * P_PAD, P_PAD), :] = prod[i * P_PAD:(i + 1) * P_PAD, lane0:lane0 + 128]

    odd = (lax.broadcasted_iota(jnp.int32, (P_PAD, gb), 1) % 2) == 1
    weights = [w_ref[t, b] for b in range(nb)]
    for p in range(size):
        s = sc_ref[pl.ds(p, gb, stride=P_PAD), :]
        tr = s.T
        row = jnp.where(odd, tr[P_PAD:2 * P_PAD], tr[0:P_PAD])
        for b in range(nb):
            acc_ref[b, p] += weights[b] * row

    @pl.when(t == pl.num_programs(0) - 1)
    def _pack():
        offs = row_offsets(size)
        for b in range(nb):
            for p in range(size):
                out_ref[b, pl.ds(offs[p], size - p), :] = acc_ref[b, p, pl.ds(p, size - p), :]


def gram_packed(tiles, weights):
    nt, size, gb, nx = tiles.shape
    nb = weights.shape[1]
    packed_rows = size * (size + 1) // 2
    return pl.pallas_call(
        gram_kernel,
        grid=(nt,),
        in_specs=[
            pl.BlockSpec(memory_space=pltpu.SMEM),
            pl.BlockSpec((None, size, gb, nx), lambda t: (t, 0, 0, 0)),
        ],
        out_specs=pl.BlockSpec((nb, packed_rows, gb), lambda t: (0, 0, 0)),
        out_shape=jax.ShapeDtypeStruct((nb, packed_rows, gb), jnp.float32),
        scratch_shapes=[
            pltpu.VMEM((nx // 128, P_PAD * gb, 128), jnp.float32),
            pltpu.VMEM((gb * P_PAD, 128), jnp.float32),
            pltpu.VMEM((nb, size, P_PAD, gb), jnp.float32),
        ],
        compiler_params=pltpu.CompilerParams(vmem_limit_bytes=48 * 1024 * 1024),
    )(weights, tiles)


def unpack_kernel(packed_ref, out_ref, u_ref):
    nb, size = out_ref.shape[0], out_ref.shape[1]
    offs = row_offsets(size)
    q_id = lax.broadcasted_iota(jnp.int32, (P_PAD, out_ref.shape[3]), 0)
    for b in range(nb):
        for p in range(size):
            u_ref[pl.ds(p * P_PAD + p, size - p), :] = packed_ref[b, pl.ds(offs[p], size - p), :]
        for p in range(size):
            up = u_ref[pl.ds(p * P_PAD, P_PAD), :]
            low = u_ref[pl.ds(p, P_PAD, stride=P_PAD), :]
            full = jnp.where(q_id >= p, up, low)
            out_ref[b, p] = full[0:size]


def unpack(packed, size):
    nb, _, gb = packed.shape
    return pl.pallas_call(
        unpack_kernel,
        in_specs=[pl.BlockSpec(memory_space=pltpu.VMEM)],
        out_specs=pl.BlockSpec(memory_space=pltpu.VMEM),
        out_shape=jax.ShapeDtypeStruct((nb, size, size, gb), jnp.float32),
        scratch_shapes=[pltpu.VMEM((P_PAD * P_PAD, gb), jnp.float32)],
    )(packed)


def local(jac, tile_count, tile_block, tile_pix, residual, direction):
    slot_total = jac.shape[1]
    blocks = direction.shape[0]
    size = jac.shape[2]
    live_count = tile_count[0, 0]
    block_ids = tile_block[0]
    pix_ids = tile_pix[0]
    alive_mask = jnp.arange(slot_total) < live_count
    alive_float = alive_mask.astype(jnp.float32)
    tiles_now = jac[0]
    block_match = block_ids[:, None] == jnp.arange(blocks)[None, :]
    block_hot = (block_match & alive_mask[:, None]).astype(jnp.float32)

    packed_gram = gram_packed(tiles_now, block_hot)
    resid_rows = jnp.take(residual[0], pix_ids, axis=0)
    grad_terms = jnp.einsum(
        "tpgx,tx->tpg", tiles_now, resid_rows, preferred_element_type=jnp.float32
    )
    grad_acc = jnp.sum(block_hot.T[:, :, None, None] * grad_terms[None], axis=1)
    payload = jnp.concatenate([packed_gram, grad_acc], axis=1)
    summed = lax.psum(payload, "view")
    packed_rows = size * (size + 1) // 2
    gram_sum = unpack(summed[:, :packed_rows], size)
    grad_sum = summed[:, packed_rows:]

    dir_rows = jnp.take(direction, block_ids, axis=0)
    shade_rows = (
        jnp.einsum("tpgx,tpg->tx", tiles_now, dir_rows, preferred_element_type=jnp.float32)
        * alive_float[:, None]
    )
    tagged = jnp.where(alive_mask, pix_ids + 1, 0).astype(jnp.float32)
    all_rows, all_tags = side_by_side((shade_rows, tagged), "gauss", 0, 1)
    own_tags = jnp.where(alive_mask, pix_ids + 1, -1).astype(jnp.float32)
    match_hot = (own_tags[:, None] == all_tags[None, :]).astype(jnp.float32)
    jp_rows = jnp.dot(match_hot, all_rows, precision=lax.Precision.HIGHEST)
    jp_round = jp_rows.astype(jnp.bfloat16)
    curv_terms = jnp.einsum("tpgx,tx->tpg", tiles_now, jp_round, preferred_element_type=jnp.float32)
    curv_acc = jnp.sum(block_hot.T[:, :, None, None] * curv_terms[None], axis=1)
    curv_sum = over_copies(curv_acc, "view")
    return (grad_sum, curv_sum, gram_sum)


def solution(mesh):
    placed = (
        P("view", "gauss", None, None, None),
        P("view", "gauss"),
        P("view", "gauss"),
        P("view", "gauss"),
        P("view", None, None),
        P("gauss", None, None),
    )
    return jax.shard_map(
        local,
        mesh=mesh,
        in_specs=placed,
        out_specs=(P("gauss", None, None), P("gauss", None, None), P("gauss", None, None, None)),
        check_vma=False,
    )
```

profile of v0, /device:TPU:1, one launch (start us, length us, event | category | flops | bytes accessed | tf_op | source)
XLA Modules:
  0.0 180.8 jit_solution(1994800629715984098)
XLA Ops:
  7.2 0.0 copy-start
  7.2 0.0 all-reduce.2.cloned.1.call-start
  7.2 0.8 compare_and_fusion
  8.0 0.7 fusion.15
  9.4 0.7 and_convert_fusion
  10.0 0.7 fusion.9.w_ref
  10.7 0.7 compare_and_fusion.1
  11.4 0.7 fusion.17
  12.1 0.7 fusion.14
  12.7 0.1 copy.20
  12.8 0.0 copy-done
  12.8 0.6 gather_fusion
  13.4 0.1 select_bitcast_fusion.1
  13.5 1.4 gather_fusion.1
  14.9 0.1 select_bitcast_fusion
  15.0 6.6 %fusion.2 = f32[4,1,256,1]{2,1,3,0:T(1,128)S(1)} fusion(bf16[4,59,128,1]{2,0,1,3:T(4,128)(2,1)S(1)} %select_bitcast_fusion, bf16[1,4,59,128,256]{4,3,2,1,0:T(8,128)(2,1)} %param.6), kind=kOutput, calls=%fused_computation.9 | convolution fusion | flops 15466496 | bytes 15531008 | tf_op jit(solution)/shard_map/tpgx,tpg->tx/dot_general | solution.py:164
  21.6 7.6 %fusion.6 = f32[4,1,59,128]{3,1,2,0:T(1,128)S(1)} fusion(bf16[4,256,1,1]{1,0,2,3:T(4,128)(2,1)S(1)} %select_bitcast_fusion.1, bf16[1,4,59,128,256]{4,3,2,1,0:T(8,128)(2,1)} %param.6), kind=kOutput, calls=%fused_computation.20 | convolution fusion | flops 15466496 | bytes 15589376 | tf_op jit(solution)/shard_map/tpgx,tx->tpg/dot_general | solution.py:152
  29.2 0.1 bitcast_multiply_fusion
  29.3 27.6 %all-gather = f32[32,4,257]{2,1,0:T(4,128)S(1)} all-gather(f32[1,4,257]{2,1,0:T(4,128)S(1)} %maximum_bitcast_fusion), channel_id=1, replica_groups=mesh['view'=4,'gauss'=32] {'gauss'}, dimensions={0}, use_global_device_ids=true | all-gather | bytes 135696 | tf_op jit(solution)/shard_map/all_gather | solution.py:17
  56.9 0.1 reshape.165
  57.0 0.1 slice_reduce_fusion
  57.1 0.2 fusion
  57.3 7.6 %fusion.4 = f32[4,1,59,128]{3,1,2,0:T(1,128)S(1)} fusion(bf16[4,256,1,1]{1,0,2,3:T(4,128)(2,1)S(1)} %fusion, bf16[1,4,59,128,256]{4,3,2,1,0:T(8,128)(2,1)} %param.6), kind=kOutput, calls=%fused_computation.18 | convolution fusion | flops 15466496 | bytes 15589376 | tf_op jit(solution)/shard_map/tpgx,tx->tpg/dot_general | solution.py:173
  64.9 37.1 %shard_map.85 = f32[2,1770,128]{2,1,0:T(8,128)S(1)} custom-call(f32[4,2]{1,0:T(4,128)S(1)} %fusion.9.w_ref, bf16[4,59,128,256]{3,2,1,0:T(8,128)(2,1)} %bitcast.49), custom_call_target="tpu_custom_call" | custom-call | tf_op jit(solution)/shard_map/pallas_call | solution.py:94
  102.0 0.4 multiply_reduce_fusion
  102.4 1.4 pad_maximum_fusion
  103.7 0.0 all-reduce.2.cloned.1.call-update
  103.8 0.1 broadcast_in_dim.44
  103.9 10.3 %all_to_all.5 = f32[4,2,59,128]{3,1,2,0:T(2,128)S(1)} all-to-all(f32[4,2,59,128]{3,1,2,0:T(2,128)S(1)} %broadcast_in_dim.44), channel_id=1, replica_groups=mesh['view'=4,'gauss'=32] {'view'}, dimensions={0} | all-to-all | bytes 483328 | tf_op jit(solution)/shard_map/all_to_all | solution.py:26
  114.2 0.7 reduce_sum.29
  114.9 42.7 %all-reduce.2.cloned.1.call-done = f32[2,1829,128]{2,1,0:T(8,128)} async-done(((f32[2,1829,128]{2,1,0:T(8,128)}), f32[2,1829,128]{2,1,0:T(8,128)}) %all-reduce.2.cloned.1.call-update) | async-done | bytes 1872912 | tf_op jit(solution)/shard_map/psum | solution.py:157
  157.6 0.8 slice.12
  158.5 0.7 copy.22
  159.1 2.8 %slice.13.packed_ref = f32[2,1770,128]{2,1,0:T(8,128)} slice(f32[2,1829,128]{2,1,0:T(8,128)} %all-reduce.2.cloned.1.call-done), slice={[0:2], [0:1770], [0:128]} | slice | bytes 3624960 | tf_op jit(solution)/shard_map/slice | solution.py:159
  162.0 4.9 %shard_map.86 = f32[2,59,59,128]{3,2,1,0:T(8,128)} custom-call(f32[2,1770,128]{2,1,0:T(8,128)} %slice.13.packed_ref), custom_call_target="tpu_custom_call" | custom-call | tf_op jit(solution)/shard_map/pallas_call | solution.py:128
  166.8 7.1 %copy.23 = f32[2,59,59,128]{3,0,2,1:T(2,128)} copy(f32[2,59,59,128]{3,2,1,0:T(8,128)} %shard_map.86) | data formatting | bytes 7129088
  (7 shorter events, 0.1 us)
Async XLA Ops:
  7.2 5.7 %copy-start = (bf16[1,4096,256]{2,1,0:T(8,128)(2,1)S(1)}, bf16[1,4096,256]{2,1,0:T(8,128)(2,1)}, u32[]{:S(2)}) copy-start(bf16[1,4096,256]{2,1,0:T(8,128)(2,1)} %param.10) | copy-start | bytes 6291460
  7.2 150.4 %all-reduce.2.cloned.1.call-start = ((), (), s32[]{:S(2)}) async-start(), calls=%async_computation.1 | async-start | bytes 3751936 | tf_op jit(solution)/shard_map/psum | solution.py:157
Sparse Core Ops, SparseCore 0:
  103.9 53.6 all-reduce.1
where the time goes:
time: 181 us
  waiting for transfers between devices  42.7 us (24%)
  Pallas kernels  41.9 us (23%)
  blocking collectives  37.9 us (21%)
  matrix products  21.9 us (12%)
  between operations  14.8 us (8%)
  local copies, waits for them, and re-layouts  13.9 us (8%)
  other arithmetic  7.55 us (4%)
    psum x1, waiting for transfers between devices, local(): summed = lax.psum(payload, 'view')  42.7 us
    pallas_call x1, Pallas kernels, gram_packed(): pl.pallas_call(gram_kernel, grid=(nt,), in_specs=[pl.BlockSpec(memory_spa...  37.1 us
    all_gather x1, blocking collectives, side_by_side(): result = lax.all_gather(both, axis, axis=dim, tiled=True)  27.6 us
    all_to_all x1, blocking collectives, copy_for_each(): lax.all_to_all(jnp.broadcast_to(array[None], (length, *array.shape)), axi...  10.3 us
    unnamed x5, local copies, waits for them, and re-layouts  7.85 us
    dot_general x1, matrix products, local(): jnp.einsum('tpgx,tx->tpg', tiles_now, jp_round, preferred_element_type=jn...  7.6 us
    dot_general x1, matrix products, local(): jnp.einsum('tpgx,tx->tpg', tiles_now, resid_rows, preferred_element_type=...  7.57 us
    dot_general x1, matrix products, local(): jnp.einsum('tpgx,tpg->tx', tiles_now, dir_rows, preferred_element_type=jn...  6.59 us
  transfers between devices with their start and end apart: 1, of which 1 were waited for; matrix products, arithmetic and copies ran while one was open for 0% of the time, Pallas kernels for 0%

commit v1 on v0

--- a/solution.py
+++ b/solution.py
@@ -154,9 +154,10 @@
     )
     grad_acc = jnp.sum(block_hot.T[:, :, None, None] * grad_terms[None], axis=1)
     payload = jnp.concatenate([packed_gram, grad_acc], axis=1)
+    payload, tiles_now = lax.optimization_barrier((payload, tiles_now))
     summed = lax.psum(payload, "view")
     packed_rows = size * (size + 1) // 2
-    gram_sum = unpack(summed[:, :packed_rows], size)
+    gram_sum = unpack(summed, size)
     grad_sum = summed[:, packed_rows:]
 
     dir_rows = jnp.take(direction, block_ids, axis=0)

time: 181 us -> 139 us (0.77)
  waiting for transfers between devices: 42.7 us -> 3.02 us
  local copies, waits for them, and re-layouts: 13.9 us -> 10.3 us
  blocking collectives: 37.9 us -> 41.1 us
  other arithmetic: 7.55 us -> 5.52 us
    psum x1, waiting for transfers between devices: 42.7 us -> 3 us  [local(): summed = lax.psum(payload, 'view')]
    all_to_all x1, blocking collectives: 10.3 us -> 13.5 us  [copy_for_each(): lax.all_to_all(jnp.broadcast_to(array[None], (length, *array.shape)), axi...]
    slice x1 -> x0, local copies, waits for them, and re-layouts: 2.83 us -> none  [local(): gram_sum = unpack(summed[:, :packed_rows], size)]
    unnamed x5 -> x11, local copies, waits for them, and re-layouts: 7.85 us -> 7.87 us
  transfers between devices with their start and end apart: 1 -> 1, of which waited for: 1 -> 1; matrix products, arithmetic and copies ran while one was open for 0% -> 12% of each run, Pallas kernels for 0% -> 0%
where the time goes in v1:
time: 139 us
  Pallas kernels  41.9 us (30%)
  blocking collectives  41.1 us (30%)
  matrix products  22.1 us (16%)
  between operations  15 us (11%)
  local copies, waits for them, and re-layouts  10.3 us (7%)
  other arithmetic  5.52 us (4%)
  waiting for transfers between devices  3.02 us (2%)
    pallas_call x1, Pallas kernels, gram_packed(): pl.pallas_call(gram_kernel, grid=(nt,), in_specs=[pl.BlockSpec(memory_spa...  37.1 us
    all_gather x1, blocking collectives, side_by_side(): result = lax.all_gather(both, axis, axis=dim, tiled=True)  27.6 us
    all_to_all x1, blocking collectives, copy_for_each(): lax.all_to_all(jnp.broadcast_to(array[None], (length, *array.shape)), axi...  13.5 us
    unnamed x11, local copies, waits for them, and re-layouts  7.87 us
    dot_general x1, matrix products, local(): jnp.einsum('tpgx,tx->tpg', tiles_now, jp_round, preferred_element_type=jn...  7.84 us
    dot_general x1, matrix products, local(): jnp.einsum('tpgx,tx->tpg', tiles_now, resid_rows, preferred_element_type=...  7.56 us
    dot_general x1, matrix products, local(): jnp.einsum('tpgx,tpg->tx', tiles_now, dir_rows, preferred_element_type=jn...  6.55 us
    pallas_call x1, Pallas kernels, unpack(): pl.pallas_call(unpack_kernel, in_specs=[pl.BlockSpec(memory_space=pltpu.V...  4.87 us
  transfers between devices with their start and end apart: 1, of which 1 were waited for; matrix products, arithmetic and copies ran while one was open for 12% of the time, Pallas kernels for 0%

profile of v1, /device:TPU:1, one launch (start us, length us, event | category | flops | bytes accessed | tf_op | source)
XLA Modules:
  0.0 139.0 jit_solution(525126859339246887)
XLA Ops:
  7.2 0.0 copy-start
  7.2 0.0 all-reduce.2.cloned.1.call-start
  8.0 0.7 and_convert_fusion
  8.7 0.7 fusion.9.w_ref
  9.4 0.7 compare_and_fusion.1
  10.1 0.7 fusion.13
  10.7 0.0 copy-done
  10.8 0.6 gather_fusion
  11.3 0.1 select_bitcast_fusion.1
  11.4 7.6 %fusion.6 = f32[4,1,59,128]{3,1,2,0:T(1,128)S(1)} fusion(bf16[4,256,1,1]{1,0,2,3:T(4,128)(2,1)S(1)} %select_bitcast_fusion.1, bf16[1,4,59,128,256]{4,3,2,1,0:T(8,128)(2,1)} %param.6), kind=kOutput, calls=%fused_computation.20 | convolution fusion | flops 15466496 | bytes 15589376 | tf_op jit(solution)/shard_map/tpgx,tx->tpg/dot_general | solution.py:152
  19.0 0.2 multiply_reduce_fusion.1
  19.2 37.1 %shard_map.85 = f32[2,1770,128]{2,1,0:T(8,128)S(1)} custom-call(f32[4,2]{1,0:T(4,128)S(1)} %fusion.9.w_ref, bf16[4,59,128,256]{3,2,1,0:T(8,128)(2,1)} %bitcast.47), custom_call_target="tpu_custom_call" | custom-call | tf_op jit(solution)/shard_map/pallas_call | solution.py:94
  56.3 0.0 copy-start.2
  56.3 0.0 copy-start.1
  56.3 1.4 pad_maximum_fusion
  57.7 0.0 all-reduce.2.cloned.1.call-update
  57.7 0.0 copy-done.2
  57.8 0.1 copy.20
  57.9 0.0 copy-done.1
  57.9 0.7 gather_fusion.1
  58.5 0.1 select_bitcast_fusion
  58.6 0.0 copy-start.3
  58.6 6.5 %fusion.2 = f32[4,1,256,1]{2,1,3,0:T(1,128)S(1)} fusion(bf16[4,59,128,256]{3,2,1,0:T(8,128)(2,1)} %bitcast.48, bf16[4,59,128,1]{2,0,1,3:T(4,128)(2,1)S(1)} %select_bitcast_fusion), kind=kOutput, calls=%fused_computation.9 | convolution fusion | flops 15466496 | bytes 15531008 | tf_op jit(solution)/shard_map/tpgx,tpg->tx/dot_general | solution.py:165
  65.2 0.1 bitcast_multiply_fusion
  65.3 27.6 %all-gather = f32[32,4,257]{2,1,0:T(4,128)S(1)} all-gather(f32[1,4,257]{2,1,0:T(4,128)S(1)} %maximum_bitcast_fusion), channel_id=1, replica_groups=mesh['view'=4,'gauss'=32] {'gauss'}, dimensions={0}, use_global_device_ids=true | all-gather | bytes 135696 | tf_op jit(solution)/shard_map/all_gather | solution.py:17
  92.9 0.1 reshape.165
  93.0 0.1 slice_reduce_fusion
  93.1 0.0 copy-done.3
  93.1 0.2 fusion
  93.3 7.8 %fusion.4 = f32[4,1,59,128]{3,1,2,0:T(1,128)S(1)} fusion(bf16[4,59,128,256]{3,2,1,0:T(8,128)(2,1)} %bitcast.49, bf16[4,256,1,1]{1,0,2,3:T(4,128)(2,1)S(1)} %fusion), kind=kOutput, calls=%fused_computation.18 | convolution fusion | flops 15466496 | bytes 15589376 | tf_op jit(solution)/shard_map/tpgx,tx->tpg/dot_general | solution.py:174
  101.2 0.2 multiply_reduce_fusion
  101.4 0.1 broadcast_in_dim.44
  101.5 13.5 %all_to_all.5 = f32[4,2,59,128]{3,1,2,0:T(2,128)S(1)} all-to-all(f32[4,2,59,128]{3,1,2,0:T(2,128)S(1)} %broadcast_in_dim.44), channel_id=1, replica_groups=mesh['view'=4,'gauss'=32] {'view'}, dimensions={0} | all-to-all | bytes 483328 | tf_op jit(solution)/shard_map/all_to_all | solution.py:26
  115.0 0.7 reduce_sum.29
  115.7 3.0 %all-reduce.2.cloned.1.call-done.packed_ref = f32[2,1829,128]{2,1,0:T(8,128)} async-done(((f32[2,1829,128]{2,1,0:T(8,128)}), f32[2,1829,128]{2,1,0:T(8,128)}) %all-reduce.2.cloned.1.call-update) | async-done | bytes 1872912 | tf_op jit(solution)/shard_map/psum | solution.py:158
  118.7 0.8 slice.8
  119.5 0.7 copy.22
  120.2 4.9 %shard_map.86 = f32[2,59,59,128]{3,2,1,0:T(8,128)} custom-call(f32[2,1829,128]{2,1,0:T(8,128)} %all-reduce.2.cloned.1.call-done.packed_ref), custom_call_target="tpu_custom_call" | custom-call | tf_op jit(solution)/shard_map/pallas_call | solution.py:128
  125.1 7.1 %copy.23 = f32[2,59,59,128]{3,0,2,1:T(2,128)} copy(f32[2,59,59,128]{3,2,1,0:T(8,128)} %shard_map.86) | data formatting | bytes 7129088
  (10 shorter events, 0.2 us)
Async XLA Ops:
  7.2 3.6 %copy-start = (bf16[1,4096,256]{2,1,0:T(8,128)(2,1)S(1)}, bf16[1,4096,256]{2,1,0:T(8,128)(2,1)}, u32[]{:S(2)}) copy-start(bf16[1,4096,256]{2,1,0:T(8,128)(2,1)} %param.10) | copy-start | bytes 6291460
  7.2 111.5 %all-reduce.2.cloned.1.call-start = ((), (), s32[]{:S(2)}) async-start(), calls=%async_computation.1 | async-start | bytes 3751936 | tf_op jit(solution)/shard_map/psum | solution.py:158
  56.3 1.4 %copy-start.2 = (s32[1,4]{1,0:T(1,128)S(1)}, s32[1,4]{1,0:T(1,128)}, u32[]{:S(2)}) copy-start(s32[1,4]{1,0:T(1,128)} %param.8) | copy-start | bytes 52
  56.3 1.5 %copy-start.1 = (bf16[2,59,128]{2,0,1:T(2,128)(2,1)S(1)}, bf16[2,59,128]{2,0,1:T(2,128)(2,1)}, u32[]{:S(2)}) copy-start(bf16[2,59,128]{2,0,1:T(2,128)(2,1)} %param.11) | copy-start | bytes 90628
  58.6 34.4 %copy-start.3 = (s32[1,4]{1,0:T(1,128)S(1)}, s32[1,4]{1,0:T(1,128)}, u32[]{:S(2)}) copy-start(s32[1,4]{1,0:T(1,128)} %param.9) | copy-start | bytes 52
Sparse Core Ops, SparseCore 0:
  57.8 60.8 all-reduce.1

commit v2 on v1

--- a/solution.py
+++ b/solution.py
@@ -110,28 +110,31 @@
 
 
 def unpack_kernel(packed_ref, out_ref, u_ref):
-    nb, size = out_ref.shape[0], out_ref.shape[1]
+    size, nb = out_ref.shape[0], out_ref.shape[2]
     offs = row_offsets(size)
     q_id = lax.broadcasted_iota(jnp.int32, (P_PAD, out_ref.shape[3]), 0)
     for b in range(nb):
         for p in range(size):
-            u_ref[pl.ds(p * P_PAD + p, size - p), :] = packed_ref[b, pl.ds(offs[p], size - p), :]
-        for p in range(size):
-            up = u_ref[pl.ds(p * P_PAD, P_PAD), :]
-            low = u_ref[pl.ds(p, P_PAD, stride=P_PAD), :]
-            full = jnp.where(q_id >= p, up, low)
-            out_ref[b, p] = full[0:size]
+            u_ref[b, pl.ds(p * P_PAD + p, size - p), :] = packed_ref[b, pl.ds(offs[p], size - p), :]
+    for p in range(size):
+        rows = []
+        for b in range(nb):
+            up = u_ref[b, pl.ds(p * P_PAD, P_PAD), :]
+            low = u_ref[b, pl.ds(p, P_PAD, stride=P_PAD), :]
+            rows.append(jnp.where(q_id >= p, up, low)[0:size])
+        out_ref[p] = jnp.stack(rows, axis=1)
 
 
 def unpack(packed, size):
     nb, _, gb = packed.shape
-    return pl.pallas_call(
+    full = pl.pallas_call(
         unpack_kernel,
         in_specs=[pl.BlockSpec(memory_space=pltpu.VMEM)],
         out_specs=pl.BlockSpec(memory_space=pltpu.VMEM),
-        out_shape=jax.ShapeDtypeStruct((nb, size, size, gb), jnp.float32),
-        scratch_shapes=[pltpu.VMEM((P_PAD * P_PAD, gb), jnp.float32)],
+        out_shape=jax.ShapeDtypeStruct((size, size, nb, gb), jnp.float32),
+        scratch_shapes=[pltpu.VMEM((nb, P_PAD * P_PAD, gb), jnp.float32)],
     )(packed)
+    return jnp.transpose(full, (2, 0, 1, 3))
 
 
 def local(jac, tile_count, tile_block, tile_pix, residual, direction):

time: 139 us -> 135 us (0.971)
  local copies, waits for them, and re-layouts: 10.3 us -> 3.23 us
  Pallas kernels: 41.9 us -> 44.6 us
    unnamed x11 -> x10, local copies, waits for them, and re-layouts: 7.87 us -> 0.77 us
    pallas_call x1, Pallas kernels: 4.87 us -> 7.52 us  [unpack(): pl.pallas_call(unpack_kernel, in_specs=[pl.BlockSpec(memory_space=pltpu.V...]
where the time goes in v2:
time: 135 us
  Pallas kernels  44.6 us (33%)
  blocking collectives  41.1 us (30%)
  matrix products  22.1 us (16%)
  between operations  15 us (11%)
  other arithmetic  5.52 us (4%)
  local copies, waits for them, and re-layouts  3.23 us (2%)
  waiting for transfers between devices  3.02 us (2%)
    pallas_call x1, Pallas kernels, gram_packed(): pl.pallas_call(gram_kernel, grid=(nt,), in_specs=[pl.BlockSpec(memory_spa...  37.1 us
    all_gather x1, blocking collectives, side_by_side(): result = lax.all_gather(both, axis, axis=dim, tiled=True)  27.6 us
    all_to_all x1, blocking collectives, copy_for_each(): lax.all_to_all(jnp.broadcast_to(array[None], (length, *array.shape)), axi...  13.5 us
    dot_general x1, matrix products, local(): jnp.einsum('tpgx,tx->tpg', tiles_now, jp_round, preferred_element_type=jn...  7.84 us
    dot_general x1, matrix products, local(): jnp.einsum('tpgx,tx->tpg', tiles_now, resid_rows, preferred_element_type=...  7.56 us
    pallas_call x1, Pallas kernels, unpack(): pl.pallas_call(unpack_kernel, in_specs=[pl.BlockSpec(memory_space=pltpu.V...  7.52 us
    dot_general x1, matrix products, local(): jnp.einsum('tpgx,tpg->tx', tiles_now, dir_rows, preferred_element_type=jn...  6.55 us
    psum x1, waiting for transfers between devices, local(): summed = lax.psum(payload, 'view')  3.01 us
  transfers between devices with their start and end apart: 1, of which 1 were waited for; matrix products, arithmetic and copies ran while one was open for 12% of the time, Pallas kernels for 0%

profile of v2, /device:TPU:1, one launch (start us, length us, event | category | flops | bytes accessed | tf_op | source)
XLA Modules:
  0.0 134.6 jit_solution(9043785641929214409)
XLA Ops:
  7.2 0.0 copy-start
  7.2 0.0 all-reduce.2.cloned.1.call-start
  8.0 0.7 and_convert_fusion
  8.7 0.7 fusion.9.w_ref
  9.4 0.7 compare_and_fusion.1
  10.1 0.7 fusion.13
  10.7 0.0 copy-done
  10.8 0.6 gather_fusion
  11.3 0.1 select_bitcast_fusion.1
  11.4 7.6 %fusion.6 = f32[4,1,59,128]{3,1,2,0:T(1,128)S(1)} fusion(bf16[4,256,1,1]{1,0,2,3:T(4,128)(2,1)S(1)} %select_bitcast_fusion.1, bf16[1,4,59,128,256]{4,3,2,1,0:T(8,128)(2,1)} %param.6), kind=kOutput, calls=%fused_computation.20 | convolution fusion | flops 15466496 | bytes 15589376 | tf_op jit(solution)/shard_map/tpgx,tx->tpg/dot_general | solution.py:155
  19.0 0.0 copy-start.2
  19.0 0.0 copy-start.1
  19.0 0.2 multiply_reduce_fusion.1
  19.3 37.1 %shard_map.85 = f32[2,1770,128]{2,1,0:T(8,128)S(1)} custom-call(f32[4,2]{1,0:T(4,128)S(1)} %fusion.9.w_ref, bf16[4,59,128,256]{3,2,1,0:T(8,128)(2,1)} %bitcast.48), custom_call_target="tpu_custom_call" | custom-call | tf_op jit(solution)/shard_map/pallas_call | solution.py:94
  56.3 0.0 copy-start.3
  56.3 1.4 %pad_maximum_fusion = f32[2,1829,128]{2,1,0:T(8,128)} fusion(f32[2,59,128]{2,1,0:T(8,128)S(1)} %multiply_reduce_fusion.1, f32[2,1770,128]{2,1,0:T(8,128)S(1)} %shard_map.85), kind=kLoop, calls=%fused_computation.2 | loop fusion | flops 468224 | bytes 3745792 | tf_op jit(solution)/shard_map/concatenate | solution.py:159
  57.7 0.0 all-reduce.2.cloned.1.call-update
  57.7 0.0 copy-done.2
  57.8 0.1 copy.16
  57.9 0.0 copy-done.1
  57.9 0.7 gather_fusion.1
  58.6 0.1 select_bitcast_fusion
  58.6 6.5 %fusion.2 = f32[4,1,256,1]{2,1,3,0:T(1,128)S(1)} fusion(bf16[4,59,128,256]{3,2,1,0:T(8,128)(2,1)} %bitcast.49, bf16[4,59,128,1]{2,0,1,3:T(4,128)(2,1)S(1)} %select_bitcast_fusion), kind=kOutput, calls=%fused_computation.9 | convolution fusion | flops 15466496 | bytes 15531008 | tf_op jit(solution)/shard_map/tpgx,tpg->tx/dot_general | solution.py:168
  65.2 0.1 bitcast_multiply_fusion
  65.3 27.6 %all-gather = f32[32,4,257]{2,1,0:T(4,128)S(1)} all-gather(f32[1,4,257]{2,1,0:T(4,128)S(1)} %maximum_bitcast_fusion), channel_id=1, replica_groups=mesh['view'=4,'gauss'=32] {'gauss'}, dimensions={0}, use_global_device_ids=true | all-gather | bytes 135696 | tf_op jit(solution)/shard_map/all_gather | solution.py:17
  92.9 0.1 reshape.165
  93.0 0.1 slice_reduce_fusion
  93.1 0.0 copy-done.3
  93.1 0.2 fusion
  93.3 7.8 %fusion.4 = f32[4,1,59,128]{3,1,2,0:T(1,128)S(1)} fusion(bf16[4,59,128,256]{3,2,1,0:T(8,128)(2,1)} %bitcast.50, bf16[4,256,1,1]{1,0,2,3:T(4,128)(2,1)S(1)} %fusion), kind=kOutput, calls=%fused_computation.18 | convolution fusion | flops 15466496 | bytes 15589376 | tf_op jit(solution)/shard_map/tpgx,tx->tpg/dot_general | solution.py:177
  101.2 0.2 multiply_reduce_fusion
  101.4 0.1 broadcast_in_dim.44
  101.5 13.5 %all_to_all.5 = f32[4,2,59,128]{3,1,2,0:T(2,128)S(1)} all-to-all(f32[4,2,59,128]{3,1,2,0:T(2,128)S(1)} %broadcast_in_dim.44), channel_id=1, replica_groups=mesh['view'=4,'gauss'=32] {'view'}, dimensions={0} | all-to-all | bytes 483328 | tf_op jit(solution)/shard_map/all_to_all | solution.py:26
  115.0 0.7 reduce_sum.29
  115.7 3.0 %all-reduce.2.cloned.1.call-done.packed_ref = f32[2,1829,128]{2,1,0:T(8,128)} async-done(((f32[2,1829,128]{2,1,0:T(8,128)}), f32[2,1829,128]{2,1,0:T(8,128)}) %all-reduce.2.cloned.1.call-update) | async-done | bytes 1872912 | tf_op jit(solution)/shard_map/psum | solution.py:161
  118.7 0.8 slice.8
  119.6 0.7 copy.18
  120.2 7.5 %shard_map.86 = f32[59,59,2,128]{3,2,1,0:T(2,128)} custom-call(f32[2,1829,128]{2,1,0:T(8,128)} %all-reduce.2.cloned.1.call-done.packed_ref), custom_call_target="tpu_custom_call" | custom-call | tf_op jit(solution)/shard_map/pallas_call | solution.py:130
  (10 shorter events, 0.2 us)
Async XLA Ops:
  7.2 3.6 %copy-start = (bf16[1,4096,256]{2,1,0:T(8,128)(2,1)S(1)}, bf16[1,4096,256]{2,1,0:T(8,128)(2,1)}, u32[]{:S(2)}) copy-start(bf16[1,4096,256]{2,1,0:T(8,128)(2,1)} %param.10) | copy-start | bytes 6291460
  7.2 111.5 %all-reduce.2.cloned.1.call-start = ((), (), s32[]{:S(2)}) async-start(), calls=%async_computation.1 | async-start | bytes 3751936 | tf_op jit(solution)/shard_map/psum | solution.py:161
  19.0 38.8 %copy-start.2 = (s32[1,4]{1,0:T(1,128)S(1)}, s32[1,4]{1,0:T(1,128)}, u32[]{:S(2)}) copy-start(s32[1,4]{1,0:T(1,128)} %param.8) | copy-start | bytes 52
  19.0 38.9 %copy-start.1 = (bf16[2,59,128]{2,0,1:T(2,128)(2,1)S(1)}, bf16[2,59,128]{2,0,1:T(2,128)(2,1)}, u32[]{:S(2)}) copy-start(bf16[2,59,128]{2,0,1:T(2,128)(2,1)} %param.11) | copy-start | bytes 90628
  56.3 36.7 %copy-start.3 = (s32[1,4]{1,0:T(1,128)S(1)}, s32[1,4]{1,0:T(1,128)}, u32[]{:S(2)}) copy-start(s32[1,4]{1,0:T(1,128)} %param.9) | copy-start | bytes 52
Sparse Core Ops, SparseCore 0:
  57.9 60.8 all-reduce.1

commit v3 on v2

--- a/solution.py
+++ b/solution.py
@@ -151,17 +151,9 @@
     block_hot = (block_match & alive_mask[:, None]).astype(jnp.float32)
 
     packed_gram = gram_packed(tiles_now, block_hot)
-    resid_rows = jnp.take(residual[0], pix_ids, axis=0)
-    grad_terms = jnp.einsum(
-        "tpgx,tx->tpg", tiles_now, resid_rows, preferred_element_type=jnp.float32
-    )
-    grad_acc = jnp.sum(block_hot.T[:, :, None, None] * grad_terms[None], axis=1)
-    payload = jnp.concatenate([packed_gram, grad_acc], axis=1)
-    payload, tiles_now = lax.optimization_barrier((payload, tiles_now))
-    summed = lax.psum(payload, "view")
-    packed_rows = size * (size + 1) // 2
+    packed_gram, tiles_now = lax.optimization_barrier((packed_gram, tiles_now))
+    summed = lax.psum(packed_gram, "view")
     gram_sum = unpack(summed, size)
-    grad_sum = summed[:, packed_rows:]
 
     dir_rows = jnp.take(direction, block_ids, axis=0)
     shade_rows = (
@@ -176,8 +168,13 @@
     jp_round = jp_rows.astype(jnp.bfloat16)
     curv_terms = jnp.einsum("tpgx,tx->tpg", tiles_now, jp_round, preferred_element_type=jnp.float32)
     curv_acc = jnp.sum(block_hot.T[:, :, None, None] * curv_terms[None], axis=1)
-    curv_sum = over_copies(curv_acc, "view")
-    return (grad_sum, curv_sum, gram_sum)
+    resid_rows = jnp.take(residual[0], pix_ids, axis=0)
+    grad_terms = jnp.einsum(
+        "tpgx,tx->tpg", tiles_now, resid_rows, preferred_element_type=jnp.float32
+    )
+    grad_acc = jnp.sum(block_hot.T[:, :, None, None] * grad_terms[None], axis=1)
+    both_sum = over_copies(jnp.stack([grad_acc, curv_acc]), "view")
+    return (both_sum[0], both_sum[1], gram_sum)
 
 
 def solution(mesh):

time: 135 us -> 128 us (0.948)
  other arithmetic: 5.52 us -> 1.65 us
  waiting for transfers between devices: 3.02 us -> 0.02 us
    psum x1, waiting for transfers between devices: 3.01 us -> 0.01 us  [local(): summed = lax.psum(packed_gram, 'view')]
    concatenate x1 -> x0, other arithmetic: 1.37 us -> none  [local(): payload = jnp.concatenate([packed_gram, grad_acc], axis=1)]
  transfers between devices with their start and end apart: 1 -> 1, of which waited for: 1 -> 0; matrix products, arithmetic and copies ran while one was open for 12% -> 20% of each run, Pallas kernels for 0% -> 0%
where the time goes in v3:
time: 128 us; the launch traced here: 127 us
  Pallas kernels  44.6 us (35%)
  blocking collectives  40 us (31%)
  matrix products  22.4 us (18%)
  between operations  15 us (12%)
  local copies, waits for them, and re-layouts  3.69 us (3%)
  other arithmetic  1.65 us (1%)
    pallas_call x1, Pallas kernels, gram_packed(): pl.pallas_call(gram_kernel, grid=(nt,), in_specs=[pl.BlockSpec(memory_spa...  37.1 us
    all_gather x1, blocking collectives, side_by_side(): result = lax.all_gather(both, axis, axis=dim, tiled=True)  27.6 us
    all_to_all x1, blocking collectives, copy_for_each(): lax.all_to_all(jnp.broadcast_to(array[None], (length, *array.shape)), axi...  12.4 us
    dot_general x1, matrix products, local(): jnp.einsum('tpgx,tx->tpg', tiles_now, resid_rows, preferred_element_type=...  7.92 us
    dot_general x1, matrix products, local(): jnp.einsum('tpgx,tx->tpg', tiles_now, jp_round, preferred_element_type=jn...  7.74 us
    pallas_call x1, Pallas kernels, unpack(): pl.pallas_call(unpack_kernel, in_specs=[pl.BlockSpec(memory_space=pltpu.V...  7.53 us
    dot_general x1, matrix products, local(): jnp.einsum('tpgx,tpg->tx', tiles_now, dir_rows, preferred_element_type=jn...  6.55 us
  transfers between devices with their start and end apart: 1, of which 0 were waited for; matrix products, arithmetic and copies ran while one was open for 20% of the time, Pallas kernels for 0%

profile of v3, /device:TPU:1, one launch (start us, length us, event | category | flops | bytes accessed | tf_op | source)
XLA Modules:
  0.0 127.4 jit_solution(14071602005672538712)
XLA Ops:
  7.2 0.0 copy-start
  7.2 0.0 copy-start.3
  7.2 0.0 copy-start.4
  7.2 0.0 copy-start.2
  7.2 0.0 all-reduce.2.cloned.1.call-start
  8.1 0.7 fusion.9.w_ref
  8.8 37.1 %shard_map.85 = f32[2,1770,128]{2,1,0:T(8,128)S(1)} custom-call(f32[4,2]{1,0:T(4,128)S(1)} %fusion.9.w_ref, bf16[4,59,128,256]{3,2,1,0:T(8,128)(2,1)} %bitcast.53), custom_call_target="tpu_custom_call" | custom-call | tf_op jit(solution)/shard_map/pallas_call | solution.py:94
  45.8 0.0 copy-start.1
  45.9 1.2 copy-done.1
  47.1 0.0 all-reduce.2.cloned.1.call-update
  47.1 0.0 copy-done.3
  47.1 0.0 copy-done.4
  47.2 0.1 copy.12
  47.3 0.0 copy-done
  47.3 0.6 gather_fusion
  47.9 0.1 select_bitcast_fusion.1
  47.9 0.0 copy-done.2
  48.0 0.7 gather_fusion.1
  48.6 0.1 select_bitcast_fusion
  48.7 6.5 %fusion.2 = f32[4,1,256,1]{2,1,3,0:T(1,128)S(1)} fusion(bf16[4,59,128,256]{3,2,1,0:T(8,128)(2,1)} %bitcast.54, bf16[4,59,128,1]{2,0,1,3:T(4,128)(2,1)S(1)} %select_bitcast_fusion), kind=kOutput, calls=%fused_computation.9 | convolution fusion | flops 15466496 | bytes 15531008 | tf_op jit(solution)/shard_map/tpgx,tpg->tx/dot_general | solution.py:160
  55.3 7.9 %fusion.6 = f32[4,1,59,128]{3,1,2,0:T(1,128)S(1)} fusion(bf16[4,59,128,256]{3,2,1,0:T(8,128)(2,1)} %bitcast.55, bf16[4,256,1,1]{1,0,2,3:T(4,128)(2,1)S(1)} %select_bitcast_fusion.1), kind=kOutput, calls=%fused_computation.22 | convolution fusion | flops 15466496 | bytes 15589376 | tf_op jit(solution)/shard_map/tpgx,tx->tpg/dot_general | solution.py:172
  63.2 0.1 bitcast_multiply_fusion
  63.3 27.6 %all-gather = f32[32,4,257]{2,1,0:T(4,128)S(1)} all-gather(f32[1,4,257]{2,1,0:T(4,128)S(1)} %maximum_bitcast_fusion), channel_id=1, replica_groups=mesh['view'=4,'gauss'=32] {'gauss'}, dimensions={0}, use_global_device_ids=true | all-gather | bytes 135696 | tf_op jit(solution)/shard_map/all_gather | solution.py:17
  90.9 0.1 reshape.165
  91.0 0.1 slice_reduce_fusion
  91.1 0.2 fusion
  91.3 7.7 %fusion.4 = f32[4,1,59,128]{3,1,2,0:T(1,128)S(1)} fusion(bf16[4,59,128,256]{3,2,1,0:T(8,128)(2,1)} %bitcast.56, bf16[4,256,1,1]{1,0,2,3:T(4,128)(2,1)S(1)} %fusion), kind=kOutput, calls=%fused_computation.20 | convolution fusion | flops 15466496 | bytes 15589376 | tf_op jit(solution)/shard_map/tpgx,tx->tpg/dot_general | solution.py:169
  99.1 0.4 multiply_reduce_fusion.1
  99.5 0.1 copy.13
  99.6 0.1 broadcast_in_dim.44
  99.7 12.4 %all_to_all.5 = f32[4,2,2,59,128]{4,2,3,1,0:T(2,128)S(1)} all-to-all(f32[4,2,2,59,128]{4,2,3,1,0:T(2,128)S(1)} %broadcast_in_dim.44), channel_id=1, replica_groups=mesh['view'=4,'gauss'=32] {'view'}, dimensions={0} | all-to-all | bytes 966656 | tf_op jit(solution)/shard_map/all_to_all | solution.py:26
  112.1 0.2 reduce_sum.29
  112.4 0.7 slice_bitcast_fusion
  113.0 0.0 all-reduce.2.cloned.1.call-done.packed_ref
  113.0 7.5 %shard_map.86 = f32[59,59,2,128]{3,2,1,0:T(2,128)} custom-call(f32[2,1770,128]{2,1,0:T(8,128)} %all-reduce.2.cloned.1.call-done.packed_ref), custom_call_target="tpu_custom_call" | custom-call | tf_op jit(solution)/shard_map/pallas_call | solution.py:130
  (13 shorter events, 0.1 us)
Async XLA Ops:
  7.2 40.1 %copy-start = (bf16[1,4096,256]{2,1,0:T(8,128)(2,1)S(1)}, bf16[1,4096,256]{2,1,0:T(8,128)(2,1)}, u32[]{:S(2)}) copy-start(bf16[1,4096,256]{2,1,0:T(8,128)(2,1)} %param.10) | copy-start | bytes 6291460
  7.2 39.9 %copy-start.3 = (s32[1,4]{1,0:T(1,128)S(1)}, s32[1,4]{1,0:T(1,128)}, u32[]{:S(2)}) copy-start(s32[1,4]{1,0:T(1,128)} %param.8) | copy-start | bytes 52
  7.2 39.9 %copy-start.4 = (s32[1,4]{1,0:T(1,128)S(1)}, s32[1,4]{1,0:T(1,128)}, u32[]{:S(2)}) copy-start(s32[1,4]{1,0:T(1,128)} %param.9) | copy-start | bytes 52
  7.2 40.7 %copy-start.2 = (bf16[2,59,128]{2,0,1:T(2,128)(2,1)S(1)}, bf16[2,59,128]{2,0,1:T(2,128)(2,1)}, u32[]{:S(2)}) copy-start(bf16[2,59,128]{2,0,1:T(2,128)(2,1)} %param.11) | copy-start | bytes 90628
  7.2 105.8 %all-reduce.2.cloned.1.call-start = ((), (), s32[]{:S(2)}) async-start(), calls=%async_computation.1 | async-start | bytes 3637248 | tf_op jit(solution)/shard_map/psum | solution.py:155
  45.8 1.2 copy-start.1
Sparse Core Ops, SparseCore 0:
  47.2 57.2 all-reduce.1

commit v4 on v3

--- a/solution.py
+++ b/solution.py
@@ -14,7 +14,7 @@
     both = jnp.concatenate(
         [a.reshape(*a.shape[:along], w) for a, w in zip(arrays, widths)], axis=along
     )
-    result = lax.all_gather(both, axis, axis=dim, tiled=True)
+    result = copy_for_each(both, axis).reshape(-1, *both.shape[1:])
     blocks = jnp.split(result, [sum(widths[:k]) for k in range(1, len(widths))], axis=along)
     return tuple(
         (b.reshape(*result.shape[:along], *a.shape[along:]) for a, b in zip(arrays, blocks))

time: 128 us -> 125 us (0.977)
  blocking collectives: 40 us -> 17.9 us
  starting transfers between devices: 0.04 us -> 9.47 us
  waiting for transfers between devices: 0.02 us -> 9.1 us
    all_gather x1 -> x0, blocking collectives: 27.6 us -> none  [side_by_side(): result = lax.all_gather(both, axis, axis=dim, tiled=True)]
    all_to_all x0 -> x1, starting transfers between devices: none -> 9.43 us  [copy_for_each(): lax.all_to_all(jnp.broadcast_to(array[None], (length, *array.shape)), axi...]
    psum x1, waiting for transfers between devices: 0.01 us -> 9.08 us  [local(): summed = lax.psum(packed_gram, 'view')]
    all_to_all x1, blocking collectives: 12.4 us -> 17.9 us  [copy_for_each(): lax.all_to_all(jnp.broadcast_to(array[None], (length, *array.shape)), axi...]
  transfers between devices with their start and end apart: 1 -> 2, of which waited for: 0 -> 1; matrix products, arithmetic and copies ran while one was open for 20% -> 21% of each run, Pallas kernels for 0% -> 0%
where the time goes in v4:
time: 125 us; the launch traced here: 124 us
  Pallas kernels  44.6 us (36%)
  matrix products  22.2 us (18%)
  blocking collectives  17.9 us (14%)
  between operations  15 us (12%)
  starting transfers between devices  9.47 us (8%)
  waiting for transfers between devices  9.1 us (7%)
  local copies, waits for them, and re-layouts  4.41 us (4%)
  other arithmetic  1.65 us (1%)
    pallas_call x1, Pallas kernels, gram_packed(): pl.pallas_call(gram_kernel, grid=(nt,), in_specs=[pl.BlockSpec(memory_spa...  37.1 us
    all_to_all x1, blocking collectives, copy_for_each(): lax.all_to_all(jnp.broadcast_to(array[None], (length, *array.shape)), axi...  17.9 us
    all_to_all x1, starting transfers between devices, copy_for_each(): lax.all_to_all(jnp.broadcast_to(array[None], (length, *array.shape)), axi...  9.43 us
    psum x1, waiting for transfers between devices, local(): summed = lax.psum(packed_gram, 'view')  9.08 us
    dot_general x1, matrix products, local(): jnp.einsum('tpgx,tx->tpg', tiles_now, resid_rows, preferred_element_type=...  7.73 us
    dot_general x1, matrix products, local(): jnp.einsum('tpgx,tx->tpg', tiles_now, jp_round, preferred_element_type=jn...  7.73 us
    pallas_call x1, Pallas kernels, unpack(): pl.pallas_call(unpack_kernel, in_specs=[pl.BlockSpec(memory_space=pltpu.V...  7.53 us
    dot_general x1, matrix products, local(): jnp.einsum('tpgx,tpg->tx', tiles_now, dir_rows, preferred_element_type=jn...  6.55 us
  transfers between devices with their start and end apart: 2, of which 1 were waited for; matrix products, arithmetic and copies ran while one was open for 21% of the time, Pallas kernels for 0%

profile of v4, /device:TPU:1, one launch (start us, length us, event | category | flops | bytes accessed | tf_op | source)
XLA Modules:
  0.0 124.3 jit_solution(8140470272412704097)
XLA Ops:
  7.2 0.0 copy-start
  7.2 0.0 copy-start.3
  7.2 0.0 copy-start.4
  7.2 0.0 copy-start.2
  7.2 0.0 all-reduce.2.cloned.1.call-start
  8.1 0.7 fusion.9.w_ref
  8.8 37.1 %shard_map.85 = f32[2,1770,128]{2,1,0:T(8,128)S(1)} custom-call(f32[4,2]{1,0:T(4,128)S(1)} %fusion.9.w_ref, bf16[4,59,128,256]{3,2,1,0:T(8,128)(2,1)} %bitcast.51), custom_call_target="tpu_custom_call" | custom-call | tf_op jit(solution)/shard_map/pallas_call | solution.py:94
  45.8 0.0 copy-start.1
  45.9 1.2 copy-done.1
  47.1 0.0 all-reduce.2.cloned.1.call-update
  47.1 0.0 copy-done.3
  47.1 0.0 copy-done.4
  47.2 0.1 copy.12
  47.3 0.0 copy-done.2
  47.3 0.7 gather_fusion.1
  47.9 0.1 select_bitcast_fusion
  48.0 6.5 %fusion.2 = f32[4,1,256,1]{2,1,3,0:T(1,128)S(1)} fusion(bf16[4,59,128,256]{3,2,1,0:T(8,128)(2,1)} %bitcast.52, bf16[4,59,128,1]{2,0,1,3:T(4,128)(2,1)S(1)} %select_bitcast_fusion), kind=kOutput, calls=%fused_computation.9 | convolution fusion | flops 15466496 | bytes 15531008 | tf_op jit(solution)/shard_map/tpgx,tpg->tx/dot_general | solution.py:160
  54.6 0.1 bitcast_multiply_fusion
  54.7 0.7 broadcast_in_dim.50
  55.4 9.4 %all-to-all-start = ((f32[32,4,257]{2,1,0:T(4,128)}), f32[32,4,257]{2,1,0:T(4,128)S(1)}, u32[]{:S(2)}, u32[]{:S(2)}) async-start(f32[32,4,257]{2,1,0:T(4,128)} %broadcast_in_dim.50), calls=%async_computation | async-start | bytes 393216 | tf_op jit(solution)/shard_map/all_to_all | solution.py:26
  64.9 0.0 copy-done
  64.9 0.6 gather_fusion
  65.4 0.1 select_bitcast_fusion.1
  65.5 7.7 %fusion.6 = f32[4,1,59,128]{3,1,2,0:T(1,128)S(1)} fusion(bf16[4,59,128,256]{3,2,1,0:T(8,128)(2,1)} %bitcast.53, bf16[4,256,1,1]{1,0,2,3:T(4,128)(2,1)S(1)} %select_bitcast_fusion.1), kind=kOutput, calls=%fused_computation.22 | convolution fusion | flops 15466496 | bytes 15589376 | tf_op jit(solution)/shard_map/tpgx,tx->tpg/dot_general | solution.py:172
  73.3 0.0 all-to-all-done
  73.3 0.1 reshape.152
  73.4 0.1 slice_reduce_fusion
  73.5 0.2 fusion
  73.7 7.7 %fusion.4 = f32[4,1,59,128]{3,1,2,0:T(1,128)S(1)} fusion(bf16[4,59,128,256]{3,2,1,0:T(8,128)(2,1)} %bitcast.54, bf16[4,256,1,1]{1,0,2,3:T(4,128)(2,1)S(1)} %fusion), kind=kOutput, calls=%fused_computation.20 | convolution fusion | flops 15466496 | bytes 15589376 | tf_op jit(solution)/shard_map/tpgx,tx->tpg/dot_general | solution.py:169
  81.5 0.4 multiply_reduce_fusion.1
  81.9 0.1 copy.13
  82.0 0.1 broadcast_in_dim.51
  82.1 17.9 %all_to_all.10 = f32[4,2,2,59,128]{4,2,3,1,0:T(2,128)S(1)} all-to-all(f32[4,2,2,59,128]{4,2,3,1,0:T(2,128)S(1)} %broadcast_in_dim.51), channel_id=1, replica_groups=mesh['view'=4,'gauss'=32] {'view'}, dimensions={0} | all-to-all | bytes 966656 | tf_op jit(solution)/shard_map/all_to_all | solution.py:26
  99.9 0.2 reduce_sum.29
  100.2 0.7 slice_bitcast_fusion
  100.8 9.1 %all-reduce.2.cloned.1.call-done.packed_ref = f32[2,1770,128]{2,1,0:T(8,128)} async-done(((f32[2,1770,128]{2,1,0:T(8,128)}), f32[2,1770,128]{2,1,0:T(8,128)}) %all-reduce.2.cloned.1.call-update) | async-done | bytes 1812496 | tf_op jit(solution)/shard_map/psum | solution.py:155
  109.9 7.5 %shard_map.86 = f32[59,59,2,128]{3,2,1,0:T(2,128)} custom-call(f32[2,1770,128]{2,1,0:T(8,128)} %all-reduce.2.cloned.1.call-done.packed_ref), custom_call_target="tpu_custom_call" | custom-call | tf_op jit(solution)/shard_map/pallas_call | solution.py:130
  (13 shorter events, 0.1 us)
Async XLA Ops:
  7.2 57.7 %copy-start = (bf16[1,4096,256]{2,1,0:T(8,128)(2,1)S(1)}, bf16[1,4096,256]{2,1,0:T(8,128)(2,1)}, u32[]{:S(2)}) copy-start(bf16[1,4096,256]{2,1,0:T(8,128)(2,1)} %param.10) | copy-start | bytes 6291460
  7.2 39.9 %copy-start.3 = (s32[1,4]{1,0:T(1,128)S(1)}, s32[1,4]{1,0:T(1,128)}, u32[]{:S(2)}) copy-start(s32[1,4]{1,0:T(1,128)} %param.8) | copy-start | bytes 52
  7.2 39.9 %copy-start.4 = (s32[1,4]{1,0:T(1,128)S(1)}, s32[1,4]{1,0:T(1,128)}, u32[]{:S(2)}) copy-start(s32[1,4]{1,0:T(1,128)} %param.9) | copy-start | bytes 52
  7.2 40.1 %copy-start.2 = (bf16[2,59,128]{2,0,1:T(2,128)(2,1)S(1)}, bf16[2,59,128]{2,0,1:T(2,128)(2,1)}, u32[]{:S(2)}) copy-start(bf16[2,59,128]{2,0,1:T(2,128)(2,1)} %param.11) | copy-start | bytes 90628
  7.2 102.7 %all-reduce.2.cloned.1.call-start = ((), (), s32[]{:S(2)}) async-start(), calls=%async_computation.2 | async-start | bytes 3637248 | tf_op jit(solution)/shard_map/psum | solution.py:155
  45.8 1.2 copy-start.1
  55.4 17.9 %all-to-all-start = ((f32[32,4,257]{2,1,0:T(4,128)}), f32[32,4,257]{2,1,0:T(4,128)S(1)}, u32[]{:S(2)}, u32[]{:S(2)}) async-start(f32[32,4,257]{2,1,0:T(4,128)} %broadcast_in_dim.50), calls=%async_computation | async-start | bytes 393216 | tf_op jit(solution)/shard_map/all_to_all | solution.py:26
Sparse Core Ops, SparseCore 0:
  47.2 62.6 all-reduce.1

commit v5 on v4

--- a/solution.py
+++ b/solution.py
@@ -34,7 +34,7 @@
 
 
 P_PAD = 64
-GROUP = 4
+GROUP = 2
 
 
 def row_offsets(size):

time: 125 us -> 124 us (level)
  no operation moved by 1% of the time
where the time goes in v5:
time: 124 us
  Pallas kernels  44.5 us (36%)
  matrix products  22.2 us (18%)
  blocking collectives  17.8 us (14%)
  between operations  15 us (12%)
  starting transfers between devices  9.47 us (8%)
  waiting for transfers between devices  9.11 us (7%)
  local copies, waits for them, and re-layouts  4.41 us (4%)
  other arithmetic  1.65 us (1%)
    pallas_call x1, Pallas kernels, gram_packed(): pl.pallas_call(gram_kernel, grid=(nt,), in_specs=[pl.BlockSpec(memory_spa...  36.9 us
    all_to_all x1, blocking collectives, copy_for_each(): lax.all_to_all(jnp.broadcast_to(array[None], (length, *array.shape)), axi...  17.8 us
    all_to_all x1, starting transfers between devices, copy_for_each(): lax.all_to_all(jnp.broadcast_to(array[None], (length, *array.shape)), axi...  9.44 us
    psum x1, waiting for transfers between devices, local(): summed = lax.psum(packed_gram, 'view')  9.09 us
    dot_general x1, matrix products, local(): jnp.einsum('tpgx,tx->tpg', tiles_now, resid_rows, preferred_element_type=...  7.73 us
    dot_general x1, matrix products, local(): jnp.einsum('tpgx,tx->tpg', tiles_now, jp_round, preferred_element_type=jn...  7.73 us
    pallas_call x1, Pallas kernels, unpack(): pl.pallas_call(unpack_kernel, in_specs=[pl.BlockSpec(memory_space=pltpu.V...  7.53 us
    dot_general x1, matrix products, local(): jnp.einsum('tpgx,tpg->tx', tiles_now, dir_rows, preferred_element_type=jn...  6.55 us
  transfers between devices with their start and end apart: 2, of which 1 were waited for; matrix products, arithmetic and copies ran while one was open for 21% of the time, Pallas kernels for 0%

profile of v5, /device:TPU:1, one launch (start us, length us, event | category | flops | bytes accessed | tf_op | source)
XLA Modules:
  0.0 124.2 jit_solution(14880639624246904279)
XLA Ops:
  7.2 0.0 copy-start
  7.2 0.0 copy-start.3
  7.2 0.0 copy-start.4
  7.2 0.0 copy-start.2
  7.2 0.0 all-reduce.2.cloned.1.call-start
  8.1 0.7 fusion.9.w_ref
  8.8 36.9 %shard_map.85 = f32[2,1770,128]{2,1,0:T(8,128)S(1)} custom-call(f32[4,2]{1,0:T(4,128)S(1)} %fusion.9.w_ref, bf16[4,59,128,256]{3,2,1,0:T(8,128)(2,1)} %bitcast.51), custom_call_target="tpu_custom_call" | custom-call | tf_op jit(solution)/shard_map/pallas_call | solution.py:94
  45.7 0.0 copy-start.1
  45.7 1.2 copy-done.1
  47.0 0.0 all-reduce.2.cloned.1.call-update
  47.0 0.0 copy-done.3
  47.0 0.0 copy-done.4
  47.0 0.1 copy.12
  47.1 0.0 copy-done.2
  47.1 0.7 gather_fusion.1
  47.8 0.1 select_bitcast_fusion
  47.9 6.5 %fusion.2 = f32[4,1,256,1]{2,1,3,0:T(1,128)S(1)} fusion(bf16[4,59,128,256]{3,2,1,0:T(8,128)(2,1)} %bitcast.52, bf16[4,59,128,1]{2,0,1,3:T(4,128)(2,1)S(1)} %select_bitcast_fusion), kind=kOutput, calls=%fused_computation.9 | convolution fusion | flops 15466496 | bytes 15531008 | tf_op jit(solution)/shard_map/tpgx,tpg->tx/dot_general | solution.py:160
  54.5 0.1 bitcast_multiply_fusion
  54.6 0.7 broadcast_in_dim.50
  55.3 9.4 %all-to-all-start = ((f32[32,4,257]{2,1,0:T(4,128)}), f32[32,4,257]{2,1,0:T(4,128)S(1)}, u32[]{:S(2)}, u32[]{:S(2)}) async-start(f32[32,4,257]{2,1,0:T(4,128)} %broadcast_in_dim.50), calls=%async_computation | async-start | bytes 393216 | tf_op jit(solution)/shard_map/all_to_all | solution.py:26
  64.8 0.0 copy-done
  64.8 0.6 gather_fusion
  65.3 0.1 select_bitcast_fusion.1
  65.4 7.7 %fusion.6 = f32[4,1,59,128]{3,1,2,0:T(1,128)S(1)} fusion(bf16[4,59,128,256]{3,2,1,0:T(8,128)(2,1)} %bitcast.53, bf16[4,256,1,1]{1,0,2,3:T(4,128)(2,1)S(1)} %select_bitcast_fusion.1), kind=kOutput, calls=%fused_computation.22 | convolution fusion | flops 15466496 | bytes 15589376 | tf_op jit(solution)/shard_map/tpgx,tx->tpg/dot_general | solution.py:172
  73.2 0.0 all-to-all-done
  73.2 0.1 reshape.152
  73.3 0.1 slice_reduce_fusion
  73.4 0.2 fusion
  73.6 7.7 %fusion.4 = f32[4,1,59,128]{3,1,2,0:T(1,128)S(1)} fusion(bf16[4,59,128,256]{3,2,1,0:T(8,128)(2,1)} %bitcast.54, bf16[4,256,1,1]{1,0,2,3:T(4,128)(2,1)S(1)} %fusion), kind=kOutput, calls=%fused_computation.20 | convolution fusion | flops 15466496 | bytes 15589376 | tf_op jit(solution)/shard_map/tpgx,tx->tpg/dot_general | solution.py:169
  81.4 0.4 multiply_reduce_fusion.1
  81.8 0.1 copy.13
  81.9 0.1 broadcast_in_dim.51
  82.0 17.8 %all_to_all.10 = f32[4,2,2,59,128]{4,2,3,1,0:T(2,128)S(1)} all-to-all(f32[4,2,2,59,128]{4,2,3,1,0:T(2,128)S(1)} %broadcast_in_dim.51), channel_id=1, replica_groups=mesh['view'=4,'gauss'=32] {'view'}, dimensions={0} | all-to-all | bytes 966656 | tf_op jit(solution)/shard_map/all_to_all | solution.py:26
  99.8 0.2 reduce_sum.29
  100.1 0.7 slice_bitcast_fusion
  100.7 9.1 %all-reduce.2.cloned.1.call-done.packed_ref = f32[2,1770,128]{2,1,0:T(8,128)} async-done(((f32[2,1770,128]{2,1,0:T(8,128)}), f32[2,1770,128]{2,1,0:T(8,128)}) %all-reduce.2.cloned.1.call-update) | async-done | bytes 1812496 | tf_op jit(solution)/shard_map/psum | solution.py:155
  109.8 7.5 %shard_map.86 = f32[59,59,2,128]{3,2,1,0:T(2,128)} custom-call(f32[2,1770,128]{2,1,0:T(8,128)} %all-reduce.2.cloned.1.call-done.packed_ref), custom_call_target="tpu_custom_call" | custom-call | tf_op jit(solution)/shard_map/pallas_call | solution.py:130
  (13 shorter events, 0.1 us)
Async XLA Ops:
  7.2 57.6 %copy-start = (bf16[1,4096,256]{2,1,0:T(8,128)(2,1)S(1)}, bf16[1,4096,256]{2,1,0:T(8,128)(2,1)}, u32[]{:S(2)}) copy-start(bf16[1,4096,256]{2,1,0:T(8,128)(2,1)} %param.10) | copy-start | bytes 6291460
  7.2 39.8 %copy-start.3 = (s32[1,4]{1,0:T(1,128)S(1)}, s32[1,4]{1,0:T(1,128)}, u32[]{:S(2)}) copy-start(s32[1,4]{1,0:T(1,128)} %param.8) | copy-start | bytes 52
  7.2 39.8 %copy-start.4 = (s32[1,4]{1,0:T(1,128)S(1)}, s32[1,4]{1,0:T(1,128)}, u32[]{:S(2)}) copy-start(s32[1,4]{1,0:T(1,128)} %param.9) | copy-start | bytes 52
  7.2 39.9 %copy-start.2 = (bf16[2,59,128]{2,0,1:T(2,128)(2,1)S(1)}, bf16[2,59,128]{2,0,1:T(2,128)(2,1)}, u32[]{:S(2)}) copy-start(bf16[2,59,128]{2,0,1:T(2,128)(2,1)} %param.11) | copy-start | bytes 90628
  7.2 102.6 %all-reduce.2.cloned.1.call-start = ((), (), s32[]{:S(2)}) async-start(), calls=%async_computation.2 | async-start | bytes 3637248 | tf_op jit(solution)/shard_map/psum | solution.py:155
  45.7 1.2 copy-start.1
  55.3 17.9 %all-to-all-start = ((f32[32,4,257]{2,1,0:T(4,128)}), f32[32,4,257]{2,1,0:T(4,128)S(1)}, u32[]{:S(2)}, u32[]{:S(2)}) async-start(f32[32,4,257]{2,1,0:T(4,128)} %broadcast_in_dim.50), calls=%async_computation | async-start | bytes 393216 | tf_op jit(solution)/shard_map/all_to_all | solution.py:26
Sparse Core Ops, SparseCore 0:
  47.1 62.6 all-reduce.1

commit v6 on v4

--- a/solution.py
+++ b/solution.py
@@ -109,28 +109,40 @@
     )(weights, tiles)
 
 
+ROW_CHUNK = 8
+
+
 def unpack_kernel(packed_ref, out_ref, u_ref):
-    size, nb = out_ref.shape[0], out_ref.shape[2]
+    step = pl.program_id(0)
+    size, nb = out_ref.shape[1], out_ref.shape[2]
     offs = row_offsets(size)
     q_id = lax.broadcasted_iota(jnp.int32, (P_PAD, out_ref.shape[3]), 0)
-    for b in range(nb):
-        for p in range(size):
-            u_ref[b, pl.ds(p * P_PAD + p, size - p), :] = packed_ref[b, pl.ds(offs[p], size - p), :]
-    for p in range(size):
-        rows = []
+
+    @pl.when(step == 0)
+    def _fill():
         for b in range(nb):
-            up = u_ref[b, pl.ds(p * P_PAD, P_PAD), :]
-            low = u_ref[b, pl.ds(p, P_PAD, stride=P_PAD), :]
-            rows.append(jnp.where(q_id >= p, up, low)[0:size])
-        out_ref[p] = jnp.stack(rows, axis=1)
+            for p in range(size):
+                u_ref[b, pl.ds(p * P_PAD + p, size - p), :] = packed_ref[b, pl.ds(offs[p], size - p), :]
+
+    for c in range(pl.cdiv(size, ROW_CHUNK)):
+        @pl.when(step == c)
+        def _rows():
+            for p in range(c * ROW_CHUNK, min(size, (c + 1) * ROW_CHUNK)):
+                rows = []
+                for b in range(nb):
+                    up = u_ref[b, pl.ds(p * P_PAD, P_PAD), :]
+                    low = u_ref[b, pl.ds(p, P_PAD, stride=P_PAD), :]
+                    rows.append(jnp.where(q_id >= p, up, low)[0:size])
+                out_ref[p - c * ROW_CHUNK] = jnp.stack(rows, axis=1)
 
 
 def unpack(packed, size):
-    nb, _, gb = packed.shape
+    nb, rows, gb = packed.shape
     full = pl.pallas_call(
         unpack_kernel,
-        in_specs=[pl.BlockSpec(memory_space=pltpu.VMEM)],
-        out_specs=pl.BlockSpec(memory_space=pltpu.VMEM),
+        grid=(pl.cdiv(size, ROW_CHUNK),),
+        in_specs=[pl.BlockSpec((nb, rows, gb), lambda i: (0, 0, 0))],
+        out_specs=pl.BlockSpec((ROW_CHUNK, size, nb, gb), lambda i: (i, 0, 0, 0)),
         out_shape=jax.ShapeDtypeStruct((size, size, nb, gb), jnp.float32),
         scratch_shapes=[pltpu.VMEM((nb, P_PAD * P_PAD, gb), jnp.float32)],
     )(packed)

time: 125 us -> 124 us (level)
  no operation moved by 1% of the time
where the time goes in v6:
time: 124 us
  Pallas kernels  44 us (35%)
  matrix products  22.2 us (18%)
  blocking collectives  17.9 us (14%)
  between operations  15 us (12%)
  starting transfers between devices  9.47 us (8%)
  waiting for transfers between devices  9.1 us (7%)
  local copies, waits for them, and re-layouts  4.41 us (4%)
  other arithmetic  1.65 us (1%)
    pallas_call x1, Pallas kernels, gram_packed(): pl.pallas_call(gram_kernel, grid=(nt,), in_specs=[pl.BlockSpec(memory_spa...  37.1 us
    all_to_all x1, blocking collectives, copy_for_each(): lax.all_to_all(jnp.broadcast_to(array[None], (length, *array.shape)), axi...  17.9 us
    all_to_all x1, starting transfers between devices, copy_for_each(): lax.all_to_all(jnp.broadcast_to(array[None], (length, *array.shape)), axi...  9.43 us
    psum x1, waiting for transfers between devices, local(): summed = lax.psum(packed_gram, 'view')  9.08 us
    dot_general x1, matrix products, local(): jnp.einsum('tpgx,tx->tpg', tiles_now, resid_rows, preferred_element_type=...  7.73 us
    dot_general x1, matrix products, local(): jnp.einsum('tpgx,tx->tpg', tiles_now, jp_round, preferred_element_type=jn...  7.73 us
    pallas_call x1, Pallas kernels, unpack(): pl.pallas_call(unpack_kernel, grid=(pl.cdiv(size, ROW_CHUNK),), in_specs=...  6.9 us
    dot_general x1, matrix products, local(): jnp.einsum('tpgx,tpg->tx', tiles_now, dir_rows, preferred_element_type=jn...  6.55 us
  transfers between devices with their start and end apart: 2, of which 1 were waited for; matrix products, arithmetic and copies ran while one was open for 21% of the time, Pallas kernels for 0%

profile of v6, /device:TPU:1, one launch (start us, length us, event | category | flops | bytes accessed | tf_op | source)
XLA Modules:
  0.0 123.7 jit_solution(1677148719045964536)
XLA Ops:
  7.2 0.0 copy-start
  7.2 0.0 copy-start.3
  7.2 0.0 copy-start.4
  7.2 0.0 copy-start.2
  7.2 0.0 all-reduce.2.cloned.1.call-start
  8.1 0.7 fusion.9.w_ref
  8.8 37.1 %shard_map.85 = f32[2,1770,128]{2,1,0:T(8,128)S(1)} custom-call(f32[4,2]{1,0:T(4,128)S(1)} %fusion.9.w_ref, bf16[4,59,128,256]{3,2,1,0:T(8,128)(2,1)} %bitcast.51), custom_call_target="tpu_custom_call" | custom-call | tf_op jit(solution)/shard_map/pallas_call | solution.py:94
  45.8 0.0 copy-start.1
  45.9 1.2 copy-done.1
  47.1 0.0 all-reduce.2.cloned.1.call-update
  47.1 0.0 copy-done.3
  47.1 0.0 copy-done.4
  47.2 0.1 copy.12
  47.3 0.0 copy-done.2
  47.3 0.7 gather_fusion.1
  47.9 0.1 select_bitcast_fusion
  48.0 6.5 %fusion.2 = f32[4,1,256,1]{2,1,3,0:T(1,128)S(1)} fusion(bf16[4,59,128,256]{3,2,1,0:T(8,128)(2,1)} %bitcast.52, bf16[4,59,128,1]{2,0,1,3:T(4,128)(2,1)S(1)} %select_bitcast_fusion), kind=kOutput, calls=%fused_computation.9 | convolution fusion | flops 15466496 | bytes 15531008 | tf_op jit(solution)/shard_map/tpgx,tpg->tx/dot_general | solution.py:172
  54.6 0.1 bitcast_multiply_fusion
  54.7 0.7 broadcast_in_dim.50
  55.4 9.4 %all-to-all-start = ((f32[32,4,257]{2,1,0:T(4,128)}), f32[32,4,257]{2,1,0:T(4,128)S(1)}, u32[]{:S(2)}, u32[]{:S(2)}) async-start(f32[32,4,257]{2,1,0:T(4,128)} %broadcast_in_dim.50), calls=%async_computation | async-start | bytes 393216 | tf_op jit(solution)/shard_map/all_to_all | solution.py:26
  64.9 0.0 copy-done
  64.9 0.6 gather_fusion
  65.4 0.1 select_bitcast_fusion.1
  65.5 7.7 %fusion.6 = f32[4,1,59,128]{3,1,2,0:T(1,128)S(1)} fusion(bf16[4,59,128,256]{3,2,1,0:T(8,128)(2,1)} %bitcast.53, bf16[4,256,1,1]{1,0,2,3:T(4,128)(2,1)S(1)} %select_bitcast_fusion.1), kind=kOutput, calls=%fused_computation.22 | convolution fusion | flops 15466496 | bytes 15589376 | tf_op jit(solution)/shard_map/tpgx,tx->tpg/dot_general | solution.py:184
  73.3 0.0 all-to-all-done
  73.3 0.1 reshape.152
  73.4 0.1 slice_reduce_fusion
  73.5 0.2 fusion
  73.7 7.7 %fusion.4 = f32[4,1,59,128]{3,1,2,0:T(1,128)S(1)} fusion(bf16[4,59,128,256]{3,2,1,0:T(8,128)(2,1)} %bitcast.54, bf16[4,256,1,1]{1,0,2,3:T(4,128)(2,1)S(1)} %fusion), kind=kOutput, calls=%fused_computation.20 | convolution fusion | flops 15466496 | bytes 15589376 | tf_op jit(solution)/shard_map/tpgx,tx->tpg/dot_general | solution.py:181
  81.5 0.4 multiply_reduce_fusion.1
  81.9 0.1 copy.13
  82.0 0.1 broadcast_in_dim.51
  82.1 17.9 %all_to_all.10 = f32[4,2,2,59,128]{4,2,3,1,0:T(2,128)S(1)} all-to-all(f32[4,2,2,59,128]{4,2,3,1,0:T(2,128)S(1)} %broadcast_in_dim.51), channel_id=1, replica_groups=mesh['view'=4,'gauss'=32] {'view'}, dimensions={0} | all-to-all | bytes 966656 | tf_op jit(solution)/shard_map/all_to_all | solution.py:26
  99.9 0.2 reduce_sum.29
  100.2 0.7 slice_bitcast_fusion
  100.8 9.1 %all-reduce.2.cloned.1.call-done.packed_ref = f32[2,1770,128]{2,1,0:T(8,128)} async-done(((f32[2,1770,128]{2,1,0:T(8,128)}), f32[2,1770,128]{2,1,0:T(8,128)}) %all-reduce.2.cloned.1.call-update) | async-done | bytes 1812496 | tf_op jit(solution)/shard_map/psum | solution.py:167
  109.9 6.9 %shard_map.86 = f32[59,59,2,128]{3,2,1,0:T(2,128)} custom-call(f32[2,1770,128]{2,1,0:T(8,128)} %all-reduce.2.cloned.1.call-done.packed_ref), custom_call_target="tpu_custom_call" | custom-call | tf_op jit(solution)/shard_map/pallas_call | solution.py:141
  (13 shorter events, 0.1 us)
Async XLA Ops:
  7.2 57.7 %copy-start = (bf16[1,4096,256]{2,1,0:T(8,128)(2,1)S(1)}, bf16[1,4096,256]{2,1,0:T(8,128)(2,1)}, u32[]{:S(2)}) copy-start(bf16[1,4096,256]{2,1,0:T(8,128)(2,1)} %param.10) | copy-start | bytes 6291460
  7.2 39.9 %copy-start.3 = (s32[1,4]{1,0:T(1,128)S(1)}, s32[1,4]{1,0:T(1,128)}, u32[]{:S(2)}) copy-start(s32[1,4]{1,0:T(1,128)} %param.8) | copy-start | bytes 52
  7.2 39.9 %copy-start.4 = (s32[1,4]{1,0:T(1,128)S(1)}, s32[1,4]{1,0:T(1,128)}, u32[]{:S(2)}) copy-start(s32[1,4]{1,0:T(1,128)} %param.9) | copy-start | bytes 52
  7.2 40.1 %copy-start.2 = (bf16[2,59,128]{2,0,1:T(2,128)(2,1)S(1)}, bf16[2,59,128]{2,0,1:T(2,128)(2,1)}, u32[]{:S(2)}) copy-start(bf16[2,59,128]{2,0,1:T(2,128)(2,1)} %param.11) | copy-start | bytes 90628
  7.2 102.7 %all-reduce.2.cloned.1.call-start = ((), (), s32[]{:S(2)}) async-start(), calls=%async_computation.2 | async-start | bytes 3637248 | tf_op jit(solution)/shard_map/psum | solution.py:167
  45.8 1.2 copy-start.1
  55.4 17.9 %all-to-all-start = ((f32[32,4,257]{2,1,0:T(4,128)}), f32[32,4,257]{2,1,0:T(4,128)S(1)}, u32[]{:S(2)}, u32[]{:S(2)}) async-start(f32[32,4,257]{2,1,0:T(4,128)} %broadcast_in_dim.50), calls=%async_computation | async-start | bytes 393216 | tf_op jit(solution)/shard_map/all_to_all | solution.py:26
Sparse Core Ops, SparseCore 0:
  47.2 62.6 all-reduce.1

commit v7 on v6

--- a/solution.py
+++ b/solution.py
@@ -46,34 +46,41 @@
     size = jac_ref.shape[0]
     gb = jac_ref.shape[1]
     nb = acc_ref.shape[0]
+    halves = xf_ref.shape[0]
+    span = P_PAD * 8
 
     @pl.when(t == 0)
     def _init():
-        for h in range(xf_ref.shape[0]):
-            xf_ref[h, pl.ds(size * gb, (P_PAD - size) * gb), :] = jnp.zeros(((P_PAD - size) * gb, 128), jnp.float32)
+        for h in range(halves):
+            for c in range(gb // 8):
+                xf_ref[h, pl.ds(c * span + size * 8, (P_PAD - size) * 8), :] = jnp.zeros(((P_PAD - size) * 8, 128), jnp.float32)
         acc_ref[...] = jnp.zeros(acc_ref.shape, jnp.float32)
 
-    halves = xf_ref.shape[0]
     for p in range(size):
         for h in range(halves):
-            xf_ref[h, pl.ds(p * gb, gb), :] = jac_ref[p, :, h * 128:(h + 1) * 128].astype(jnp.float32)
+            slab = jac_ref[p, :, h * 128:(h + 1) * 128].astype(jnp.float32)
+            for c in range(gb // 8):
+                xf_ref[h, pl.ds(c * span + p * 8, 8), :] = slab[c * 8:(c + 1) * 8]
 
     for c in range(gb // GROUP):
-        parts = [
-            jnp.concatenate([xf_ref[h, pl.ds(c * GROUP + i, P_PAD, stride=gb), :] for h in range(halves)], axis=1)
-            for i in range(GROUP)
-        ]
+        parts = []
+        for i in range(GROUP):
+            g = c * GROUP + i
+            base = (g // 8) * span + g % 8
+            parts.append(jnp.concatenate([xf_ref[h, pl.ds(base, P_PAD, stride=8), :] for h in range(halves)], axis=1))
         a = jnp.concatenate(parts, axis=0).astype(jnp.bfloat16)
         prod = lax.dot_general(a, a, (((1,), (1,)), ((), ())), preferred_element_type=jnp.float32)
         for i in range(GROUP):
             g = c * GROUP + i
             lane0 = 128 * ((i * P_PAD) // 128)
-            sc_ref[pl.ds(g * P_PAD, P_PAD), :] = prod[i * P_PAD:(i + 1) * P_PAD, lane0:lane0 + 128]
+            block = prod[i * P_PAD:(i + 1) * P_PAD, lane0:lane0 + 128]
+            for r in range(P_PAD // 8):
+                sc_ref[pl.ds(r * gb * 8 + g * 8, 8), :] = block[r * 8:(r + 1) * 8]
 
     odd = (lax.broadcasted_iota(jnp.int32, (P_PAD, gb), 1) % 2) == 1
     weights = [w_ref[t, b] for b in range(nb)]
     for p in range(size):
-        s = sc_ref[pl.ds(p, gb, stride=P_PAD), :]
+        s = sc_ref[pl.ds((p // 8) * gb * 8 + p % 8, gb, stride=8), :]
         tr = s.T
         row = jnp.where(odd, tr[P_PAD:2 * P_PAD], tr[0:P_PAD])
         for b in range(nb):

time: 124 us -> 104 us (0.84)
  Pallas kernels: 44 us -> 24 us
    pallas_call x1, Pallas kernels: 37.1 us -> 17.1 us  [gram_packed(): pl.pallas_call(gram_kernel, grid=(nt,), in_specs=[pl.BlockSpec(memory_spa...]
  transfers between devices with their start and end apart: 2 -> 2, of which waited for: 1 -> 1; matrix products, arithmetic and copies ran while one was open for 21% -> 25% of each run, Pallas kernels for 0% -> 0%
where the time goes in v7:
time: 104 us
  Pallas kernels  24 us (23%)
  matrix products  22.2 us (21%)
  blocking collectives  17.8 us (17%)
  between operations  15 us (14%)
  starting transfers between devices  9.46 us (9%)
  waiting for transfers between devices  9.12 us (9%)
  local copies, waits for them, and re-layouts  4.41 us (4%)
  other arithmetic  1.65 us (2%)
    all_to_all x1, blocking collectives, copy_for_each(): lax.all_to_all(jnp.broadcast_to(array[None], (length, *array.shape)), axi...  17.8 us
    pallas_call x1, Pallas kernels, gram_packed(): pl.pallas_call(gram_kernel, grid=(nt,), in_specs=[pl.BlockSpec(memory_spa...  17.1 us
    all_to_all x1, starting transfers between devices, copy_for_each(): lax.all_to_all(jnp.broadcast_to(array[None], (length, *array.shape)), axi...  9.42 us
    psum x1, waiting for transfers between devices, local(): summed = lax.psum(packed_gram, 'view')  9.1 us
    dot_general x1, matrix products, local(): jnp.einsum('tpgx,tx->tpg', tiles_now, resid_rows, preferred_element_type=...  7.73 us
    dot_general x1, matrix products, local(): jnp.einsum('tpgx,tx->tpg', tiles_now, jp_round, preferred_element_type=jn...  7.73 us
    pallas_call x1, Pallas kernels, unpack(): pl.pallas_call(unpack_kernel, grid=(pl.cdiv(size, ROW_CHUNK),), in_specs=...  6.9 us
    dot_general x1, matrix products, local(): jnp.einsum('tpgx,tpg->tx', tiles_now, dir_rows, preferred_element_type=jn...  6.55 us
  transfers between devices with their start and end apart: 2, of which 1 were waited for; matrix products, arithmetic and copies ran while one was open for 25% of the time, Pallas kernels for 0%

profile of v7, /device:TPU:1, one launch (start us, length us, event | category | flops | bytes accessed | tf_op | source)
XLA Modules:
  0.0 103.7 jit_solution(7235491342195942308)
XLA Ops:
  7.2 0.0 copy-start
  7.2 0.0 copy-start.3
  7.2 0.0 copy-start.4
  7.2 0.0 copy-start.2
  7.2 0.0 all-reduce.2.cloned.1.call-start
  8.1 0.7 fusion.9.w_ref
  8.8 17.1 %shard_map.85 = f32[2,1770,128]{2,1,0:T(8,128)S(1)} custom-call(f32[4,2]{1,0:T(4,128)S(1)} %fusion.9.w_ref, bf16[4,59,128,256]{3,2,1,0:T(8,128)(2,1)} %bitcast.51), custom_call_target="tpu_custom_call" | custom-call | tf_op jit(solution)/shard_map/pallas_call | solution.py:101
  25.8 0.0 copy-start.1
  25.9 1.2 %copy-done.1 = f32[2,1770,128]{2,1,0:T(8,128)} copy-done((f32[2,1770,128]{2,1,0:T(8,128)}, f32[2,1770,128]{2,1,0:T(8,128)S(1)}, u32[]{:S(2)}) %copy-start.1) | copy-done | bytes 1812504
  27.1 0.0 all-reduce.2.cloned.1.call-update
  27.1 0.0 copy-done.3
  27.1 0.0 copy-done.4
  27.2 0.1 copy.12
  27.3 0.0 copy-done.2
  27.3 0.7 gather_fusion.1
  27.9 0.1 select_bitcast_fusion
  28.0 6.5 %fusion.2 = f32[4,1,256,1]{2,1,3,0:T(1,128)S(1)} fusion(bf16[4,59,128,256]{3,2,1,0:T(8,128)(2,1)} %bitcast.52, bf16[4,59,128,1]{2,0,1,3:T(4,128)(2,1)S(1)} %select_bitcast_fusion), kind=kOutput, calls=%fused_computation.9 | convolution fusion | flops 15466496 | bytes 15531008 | tf_op jit(solution)/shard_map/tpgx,tpg->tx/dot_general | solution.py:179
  34.6 0.1 bitcast_multiply_fusion
  34.7 0.7 broadcast_in_dim.50
  35.4 9.4 %all-to-all-start = ((f32[32,4,257]{2,1,0:T(4,128)}), f32[32,4,257]{2,1,0:T(4,128)S(1)}, u32[]{:S(2)}, u32[]{:S(2)}) async-start(f32[32,4,257]{2,1,0:T(4,128)} %broadcast_in_dim.50), calls=%async_computation | async-start | bytes 393216 | tf_op jit(solution)/shard_map/all_to_all | solution.py:26
  44.8 0.0 copy-done
  44.9 0.6 gather_fusion
  45.4 0.1 select_bitcast_fusion.1
  45.5 7.7 %fusion.6 = f32[4,1,59,128]{3,1,2,0:T(1,128)S(1)} fusion(bf16[4,59,128,256]{3,2,1,0:T(8,128)(2,1)} %bitcast.53, bf16[4,256,1,1]{1,0,2,3:T(4,128)(2,1)S(1)} %select_bitcast_fusion.1), kind=kOutput, calls=%fused_computation.22 | convolution fusion | flops 15466496 | bytes 15589376 | tf_op jit(solution)/shard_map/tpgx,tx->tpg/dot_general | solution.py:191
  53.3 0.0 all-to-all-done
  53.3 0.1 reshape.152
  53.4 0.1 slice_reduce_fusion
  53.5 0.2 fusion
  53.7 7.7 %fusion.4 = f32[4,1,59,128]{3,1,2,0:T(1,128)S(1)} fusion(bf16[4,59,128,256]{3,2,1,0:T(8,128)(2,1)} %bitcast.54, bf16[4,256,1,1]{1,0,2,3:T(4,128)(2,1)S(1)} %fusion), kind=kOutput, calls=%fused_computation.20 | convolution fusion | flops 15466496 | bytes 15589376 | tf_op jit(solution)/shard_map/tpgx,tx->tpg/dot_general | solution.py:188
  61.5 0.4 multiply_reduce_fusion.1
  61.8 0.1 copy.13
  61.9 0.1 broadcast_in_dim.51
  62.1 17.8 %all_to_all.10 = f32[4,2,2,59,128]{4,2,3,1,0:T(2,128)S(1)} all-to-all(f32[4,2,2,59,128]{4,2,3,1,0:T(2,128)S(1)} %broadcast_in_dim.51), channel_id=1, replica_groups=mesh['view'=4,'gauss'=32] {'view'}, dimensions={0} | all-to-all | bytes 966656 | tf_op jit(solution)/shard_map/all_to_all | solution.py:26
  79.9 0.2 reduce_sum.29
  80.2 0.7 slice_bitcast_fusion
  80.8 9.1 %all-reduce.2.cloned.1.call-done.packed_ref = f32[2,1770,128]{2,1,0:T(8,128)} async-done(((f32[2,1770,128]{2,1,0:T(8,128)}), f32[2,1770,128]{2,1,0:T(8,128)}) %all-reduce.2.cloned.1.call-update) | async-done | bytes 1812496 | tf_op jit(solution)/shard_map/psum | solution.py:174
  89.9 6.9 %shard_map.86 = f32[59,59,2,128]{3,2,1,0:T(2,128)} custom-call(f32[2,1770,128]{2,1,0:T(8,128)} %all-reduce.2.cloned.1.call-done.packed_ref), custom_call_target="tpu_custom_call" | custom-call | tf_op jit(solution)/shard_map/pallas_call | solution.py:148
  (13 shorter events, 0.1 us)
Async XLA Ops:
  7.2 37.7 %copy-start = (bf16[1,4096,256]{2,1,0:T(8,128)(2,1)S(1)}, bf16[1,4096,256]{2,1,0:T(8,128)(2,1)}, u32[]{:S(2)}) copy-start(bf16[1,4096,256]{2,1,0:T(8,128)(2,1)} %param.10) | copy-start | bytes 6291460
  7.2 19.9 %copy-start.3 = (s32[1,4]{1,0:T(1,128)S(1)}, s32[1,4]{1,0:T(1,128)}, u32[]{:S(2)}) copy-start(s32[1,4]{1,0:T(1,128)} %param.8) | copy-start | bytes 52
  7.2 19.9 %copy-start.4 = (s32[1,4]{1,0:T(1,128)S(1)}, s32[1,4]{1,0:T(1,128)}, u32[]{:S(2)}) copy-start(s32[1,4]{1,0:T(1,128)} %param.9) | copy-start | bytes 52
  7.2 20.1 %copy-start.2 = (bf16[2,59,128]{2,0,1:T(2,128)(2,1)S(1)}, bf16[2,59,128]{2,0,1:T(2,128)(2,1)}, u32[]{:S(2)}) copy-start(bf16[2,59,128]{2,0,1:T(2,128)(2,1)} %param.11) | copy-start | bytes 90628
  7.2 82.7 %all-reduce.2.cloned.1.call-start = ((), (), s32[]{:S(2)}) async-start(), calls=%async_computation.2 | async-start | bytes 3637248 | tf_op jit(solution)/shard_map/psum | solution.py:174
  25.8 1.2 %copy-start.1 = (f32[2,1770,128]{2,1,0:T(8,128)}, f32[2,1770,128]{2,1,0:T(8,128)S(1)}, u32[]{:S(2)}) copy-start(f32[2,1770,128]{2,1,0:T(8,128)S(1)} %shard_map.85) | copy-start | bytes 5437444
  35.4 17.9 %all-to-all-start = ((f32[32,4,257]{2,1,0:T(4,128)}), f32[32,4,257]{2,1,0:T(4,128)S(1)}, u32[]{:S(2)}, u32[]{:S(2)}) async-start(f32[32,4,257]{2,1,0:T(4,128)} %broadcast_in_dim.50), calls=%async_computation | async-start | bytes 393216 | tf_op jit(solution)/shard_map/all_to_all | solution.py:26
Sparse Core Ops, SparseCore 0:
  27.2 62.6 all-reduce.1

commit v8 on v7

--- a/solution.py
+++ b/solution.py
@@ -123,13 +123,17 @@
     step = pl.program_id(0)
     size, nb = out_ref.shape[1], out_ref.shape[2]
     offs = row_offsets(size)
+    span = P_PAD * 8
     q_id = lax.broadcasted_iota(jnp.int32, (P_PAD, out_ref.shape[3]), 0)
 
     @pl.when(step == 0)
     def _fill():
         for b in range(nb):
             for p in range(size):
-                u_ref[b, pl.ds(p * P_PAD + p, size - p), :] = packed_ref[b, pl.ds(offs[p], size - p), :]
+                for qb in range(p // 8, pl.cdiv(size, 8)):
+                    q0 = max(p, qb * 8)
+                    q1 = min(size, qb * 8 + 8)
+                    u_ref[b, pl.ds(qb * span + p * 8 + q0 % 8, q1 - q0), :] = packed_ref[b, pl.ds(offs[p] + q0 - p, q1 - q0), :]
 
     for c in range(pl.cdiv(size, ROW_CHUNK)):
         @pl.when(step == c)
@@ -137,8 +141,8 @@
             for p in range(c * ROW_CHUNK, min(size, (c + 1) * ROW_CHUNK)):
                 rows = []
                 for b in range(nb):
-                    up = u_ref[b, pl.ds(p * P_PAD, P_PAD), :]
-                    low = u_ref[b, pl.ds(p, P_PAD, stride=P_PAD), :]
+                    up = jnp.concatenate([u_ref[b, pl.ds(qb * span + p * 8, 8), :] for qb in range(P_PAD // 8)], axis=0)
+                    low = u_ref[b, pl.ds((p // 8) * span + p % 8, P_PAD, stride=8), :]
                     rows.append(jnp.where(q_id >= p, up, low)[0:size])
                 out_ref[p - c * ROW_CHUNK] = jnp.stack(rows, axis=1)
 

time: 104 us -> 103 us (level)
  no operation moved by 1% of the time
where the time goes in v8:
time: 103 us
  Pallas kernels  23.4 us (23%)
  matrix products  22.2 us (22%)
  blocking collectives  17.8 us (17%)
  between operations  15 us (15%)
  starting transfers between devices  9.46 us (9%)
  waiting for transfers between devices  9.12 us (9%)
  local copies, waits for them, and re-layouts  4.41 us (4%)
  other arithmetic  1.65 us (2%)
    all_to_all x1, blocking collectives, copy_for_each(): lax.all_to_all(jnp.broadcast_to(array[None], (length, *array.shape)), axi...  17.8 us
    pallas_call x1, Pallas kernels, gram_packed(): pl.pallas_call(gram_kernel, grid=(nt,), in_specs=[pl.BlockSpec(memory_spa...  17.1 us
    all_to_all x1, starting transfers between devices, copy_for_each(): lax.all_to_all(jnp.broadcast_to(array[None], (length, *array.shape)), axi...  9.42 us
    psum x1, waiting for transfers between devices, local(): summed = lax.psum(packed_gram, 'view')  9.1 us
    dot_general x1, matrix products, local(): jnp.einsum('tpgx,tx->tpg', tiles_now, resid_rows, preferred_element_type=...  7.73 us
    dot_general x1, matrix products, local(): jnp.einsum('tpgx,tx->tpg', tiles_now, jp_round, preferred_element_type=jn...  7.73 us
    dot_general x1, matrix products, local(): jnp.einsum('tpgx,tpg->tx', tiles_now, dir_rows, preferred_element_type=jn...  6.55 us
    pallas_call x1, Pallas kernels, unpack(): pl.pallas_call(unpack_kernel, grid=(pl.cdiv(size, ROW_CHUNK),), in_specs=...  6.34 us
  transfers between devices with their start and end apart: 2, of which 1 were waited for; matrix products, arithmetic and copies ran while one was open for 25% of the time, Pallas kernels for 0%

profile of v8, /device:TPU:1, one launch (start us, length us, event | category | flops | bytes accessed | tf_op | source)
XLA Modules:
  0.0 103.1 jit_solution(14829849141999461760)
XLA Ops:
  7.2 0.0 copy-start
  7.2 0.0 copy-start.3
  7.2 0.0 copy-start.4
  7.2 0.0 copy-start.2
  7.2 0.0 all-reduce.2.cloned.1.call-start
  8.1 0.7 fusion.9.w_ref
  8.8 17.1 %shard_map.85 = f32[2,1770,128]{2,1,0:T(8,128)S(1)} custom-call(f32[4,2]{1,0:T(4,128)S(1)} %fusion.9.w_ref, bf16[4,59,128,256]{3,2,1,0:T(8,128)(2,1)} %bitcast.51), custom_call_target="tpu_custom_call" | custom-call | tf_op jit(solution)/shard_map/pallas_call | solution.py:101
  25.8 0.0 copy-start.1
  25.9 1.2 %copy-done.1 = f32[2,1770,128]{2,1,0:T(8,128)} copy-done((f32[2,1770,128]{2,1,0:T(8,128)}, f32[2,1770,128]{2,1,0:T(8,128)S(1)}, u32[]{:S(2)}) %copy-start.1) | copy-done | bytes 1812504
  27.1 0.0 all-reduce.2.cloned.1.call-update
  27.1 0.0 copy-done.3
  27.1 0.0 copy-done.4
  27.2 0.1 copy.12
  27.3 0.0 copy-done.2
  27.3 0.7 gather_fusion.1
  27.9 0.1 select_bitcast_fusion
  28.0 6.5 %fusion.2 = f32[4,1,256,1]{2,1,3,0:T(1,128)S(1)} fusion(bf16[4,59,128,256]{3,2,1,0:T(8,128)(2,1)} %bitcast.52, bf16[4,59,128,1]{2,0,1,3:T(4,128)(2,1)S(1)} %select_bitcast_fusion), kind=kOutput, calls=%fused_computation.9 | convolution fusion | flops 15466496 | bytes 15531008 | tf_op jit(solution)/shard_map/tpgx,tpg->tx/dot_general | solution.py:183
  34.6 0.1 bitcast_multiply_fusion
  34.7 0.7 broadcast_in_dim.50
  35.4 9.4 %all-to-all-start = ((f32[32,4,257]{2,1,0:T(4,128)}), f32[32,4,257]{2,1,0:T(4,128)S(1)}, u32[]{:S(2)}, u32[]{:S(2)}) async-start(f32[32,4,257]{2,1,0:T(4,128)} %broadcast_in_dim.50), calls=%async_computation | async-start | bytes 393216 | tf_op jit(solution)/shard_map/all_to_all | solution.py:26
  44.8 0.0 copy-done
  44.9 0.6 gather_fusion
  45.4 0.1 select_bitcast_fusion.1
  45.5 7.7 %fusion.6 = f32[4,1,59,128]{3,1,2,0:T(1,128)S(1)} fusion(bf16[4,59,128,256]{3,2,1,0:T(8,128)(2,1)} %bitcast.53, bf16[4,256,1,1]{1,0,2,3:T(4,128)(2,1)S(1)} %select_bitcast_fusion.1), kind=kOutput, calls=%fused_computation.22 | convolution fusion | flops 15466496 | bytes 15589376 | tf_op jit(solution)/shard_map/tpgx,tx->tpg/dot_general | solution.py:195
  53.3 0.0 all-to-all-done
  53.3 0.1 reshape.152
  53.4 0.1 slice_reduce_fusion
  53.5 0.2 fusion
  53.7 7.7 %fusion.4 = f32[4,1,59,128]{3,1,2,0:T(1,128)S(1)} fusion(bf16[4,59,128,256]{3,2,1,0:T(8,128)(2,1)} %bitcast.54, bf16[4,256,1,1]{1,0,2,3:T(4,128)(2,1)S(1)} %fusion), kind=kOutput, calls=%fused_computation.20 | convolution fusion | flops 15466496 | bytes 15589376 | tf_op jit(solution)/shard_map/tpgx,tx->tpg/dot_general | solution.py:192
  61.5 0.4 multiply_reduce_fusion.1
  61.8 0.1 copy.13
  61.9 0.1 broadcast_in_dim.51
  62.1 17.8 %all_to_all.10 = f32[4,2,2,59,128]{4,2,3,1,0:T(2,128)S(1)} all-to-all(f32[4,2,2,59,128]{4,2,3,1,0:T(2,128)S(1)} %broadcast_in_dim.51), channel_id=1, replica_groups=mesh['view'=4,'gauss'=32] {'view'}, dimensions={0} | all-to-all | bytes 966656 | tf_op jit(solution)/shard_map/all_to_all | solution.py:26
  79.9 0.2 reduce_sum.29
  80.2 0.7 slice_bitcast_fusion
  80.8 9.1 %all-reduce.2.cloned.1.call-done.packed_ref = f32[2,1770,128]{2,1,0:T(8,128)} async-done(((f32[2,1770,128]{2,1,0:T(8,128)}), f32[2,1770,128]{2,1,0:T(8,128)}) %all-reduce.2.cloned.1.call-update) | async-done | bytes 1812496 | tf_op jit(solution)/shard_map/psum | solution.py:178
  89.9 6.3 %shard_map.86 = f32[59,59,2,128]{3,2,1,0:T(2,128)} custom-call(f32[2,1770,128]{2,1,0:T(8,128)} %all-reduce.2.cloned.1.call-done.packed_ref), custom_call_target="tpu_custom_call" | custom-call | tf_op jit(solution)/shard_map/pallas_call | solution.py:152
  (13 shorter events, 0.1 us)
Async XLA Ops:
  7.2 37.7 %copy-start = (bf16[1,4096,256]{2,1,0:T(8,128)(2,1)S(1)}, bf16[1,4096,256]{2,1,0:T(8,128)(2,1)}, u32[]{:S(2)}) copy-start(bf16[1,4096,256]{2,1,0:T(8,128)(2,1)} %param.10) | copy-start | bytes 6291460
  7.2 19.9 %copy-start.3 = (s32[1,4]{1,0:T(1,128)S(1)}, s32[1,4]{1,0:T(1,128)}, u32[]{:S(2)}) copy-start(s32[1,4]{1,0:T(1,128)} %param.8) | copy-start | bytes 52
  7.2 19.9 %copy-start.4 = (s32[1,4]{1,0:T(1,128)S(1)}, s32[1,4]{1,0:T(1,128)}, u32[]{:S(2)}) copy-start(s32[1,4]{1,0:T(1,128)} %param.9) | copy-start | bytes 52
  7.2 20.1 %copy-start.2 = (bf16[2,59,128]{2,0,1:T(2,128)(2,1)S(1)}, bf16[2,59,128]{2,0,1:T(2,128)(2,1)}, u32[]{:S(2)}) copy-start(bf16[2,59,128]{2,0,1:T(2,128)(2,1)} %param.11) | copy-start | bytes 90628
  7.2 82.7 %all-reduce.2.cloned.1.call-start = ((), (), s32[]{:S(2)}) async-start(), calls=%async_computation.2 | async-start | bytes 3637248 | tf_op jit(solution)/shard_map/psum | solution.py:178
  25.8 1.2 %copy-start.1 = (f32[2,1770,128]{2,1,0:T(8,128)}, f32[2,1770,128]{2,1,0:T(8,128)S(1)}, u32[]{:S(2)}) copy-start(f32[2,1770,128]{2,1,0:T(8,128)S(1)} %shard_map.85) | copy-start | bytes 5437444
  35.4 17.9 %all-to-all-start = ((f32[32,4,257]{2,1,0:T(4,128)}), f32[32,4,257]{2,1,0:T(4,128)S(1)}, u32[]{:S(2)}, u32[]{:S(2)}) async-start(f32[32,4,257]{2,1,0:T(4,128)} %broadcast_in_dim.50), calls=%async_computation | async-start | bytes 393216 | tf_op jit(solution)/shard_map/all_to_all | solution.py:26
Sparse Core Ops, SparseCore 0:
  27.2 62.6 all-reduce.1

commit v9 on v8

--- a/solution.py
+++ b/solution.py
@@ -89,7 +89,9 @@
     @pl.when(t == pl.num_programs(0) - 1)
     def _pack():
         offs = row_offsets(size)
+        tail = out_ref.shape[1] - size * (size + 1) // 2
         for b in range(nb):
+            out_ref[b, pl.ds(out_ref.shape[1] - tail, tail), :] = jnp.zeros((tail, out_ref.shape[2]), jnp.float32)
             for p in range(size):
                 out_ref[b, pl.ds(offs[p], size - p), :] = acc_ref[b, p, pl.ds(p, size - p), :]
 
@@ -97,7 +99,7 @@
 def gram_packed(tiles, weights):
     nt, size, gb, nx = tiles.shape
     nb = weights.shape[1]
-    packed_rows = size * (size + 1) // 2
+    packed_rows = -(-(size * (size + 1) // 2) // 8) * 8
     return pl.pallas_call(
         gram_kernel,
         grid=(nt,),
@@ -175,7 +177,10 @@
 
     packed_gram = gram_packed(tiles_now, block_hot)
     packed_gram, tiles_now = lax.optimization_barrier((packed_gram, tiles_now))
-    summed = lax.psum(packed_gram, "view")
+    parts = lax.axis_size("view")
+    chunks = packed_gram.reshape(parts, -1, packed_gram.shape[2])
+    mine = jnp.sum(lax.all_to_all(chunks, "view", 0, 0, tiled=True), axis=0)
+    summed = copy_for_each(mine, "view").reshape(packed_gram.shape)
     gram_sum = unpack(summed, size)
 
     dir_rows = jnp.take(direction, block_ids, axis=0)

time: 103 us -> 124 us (1.20); the launches traced: 103 us -> 121 us
  waiting for transfers between devices: 9.12 us -> 40.7 us
  blocking collectives: 17.8 us -> 0 us
  between operations: 15 us -> 1.51 us
  starting transfers between devices: 9.46 us -> 21.9 us
  other arithmetic: 1.65 us -> 5.42 us
  local copies, waits for them, and re-layouts: 4.41 us -> 6.51 us
    all_to_all x1 -> x3, waiting for transfers between devices: 0.01 us -> 26 us  [copy_for_each(): lax.all_to_all(jnp.broadcast_to(array[None], (length, *array.shape)), axi...]
    all_to_all x1 -> x0, blocking collectives: 17.8 us -> none  [copy_for_each(): lax.all_to_all(jnp.broadcast_to(array[None], (length, *array.shape)), axi...]
    all_to_all x0 -> x1, waiting for transfers between devices: none -> 14.6 us  [local(): mine = jnp.sum(lax.all_to_all(chunks, 'view', 0, 0, tiled=True), axis=0)]
    psum x1 -> x0, waiting for transfers between devices: 9.1 us -> none  [local(): summed = lax.psum(packed_gram, 'view')]
    all_to_all x1 -> x3, starting transfers between devices: 9.42 us -> 17.5 us  [copy_for_each(): lax.all_to_all(jnp.broadcast_to(array[None], (length, *array.shape)), axi...]
    all_to_all x0 -> x1, starting transfers between devices: none -> 4.41 us  [local(): mine = jnp.sum(lax.all_to_all(chunks, 'view', 0, 0, tiled=True), axis=0)]
    broadcast_in_dim x2 -> x3, local copies, waits for them, and re-layouts: 0.84 us -> 2.94 us  [copy_for_each(): jnp.broadcast_to(array[None], (length, *array.shape))]
    reduce_sum x0 -> x1, other arithmetic: none -> 1.66 us  [local(): mine = jnp.sum(lax.all_to_all(chunks, 'view', 0, 0, tiled=True), axis=0)]
  transfers between devices with their start and end apart: 2 -> 4, of which waited for: 1 -> 3; matrix products, arithmetic and copies ran while one was open for 25% -> 16% of each run, Pallas kernels for 0% -> 0%
where the time goes in v9:
time: 124 us; the launch traced here: 121 us
  waiting for transfers between devices  40.7 us (33%)
  Pallas kernels  23.4 us (19%)
  matrix products  21.9 us (18%)
  starting transfers between devices  21.9 us (18%)
  local copies, waits for them, and re-layouts  6.51 us (5%)
  other arithmetic  5.42 us (4%)
  between operations  1.51 us (1%)
    all_to_all x3, waiting for transfers between devices, copy_for_each(): lax.all_to_all(jnp.broadcast_to(array[None], (length, *array.shape)), axi...  26 us
    all_to_all x3, starting transfers between devices, copy_for_each(): lax.all_to_all(jnp.broadcast_to(array[None], (length, *array.shape)), axi...  17.5 us
    pallas_call x1, Pallas kernels, gram_packed(): pl.pallas_call(gram_kernel, grid=(nt,), in_specs=[pl.BlockSpec(memory_spa...  17.1 us
    all_to_all x1, waiting for transfers between devices, local(): mine = jnp.sum(lax.all_to_all(chunks, 'view', 0, 0, tiled=True), axis=0)  14.6 us
    dot_general x1, matrix products, local(): jnp.einsum('tpgx,tx->tpg', tiles_now, jp_round, preferred_element_type=jn...  7.6 us
    dot_general x1, matrix products, local(): jnp.einsum('tpgx,tx->tpg', tiles_now, resid_rows, preferred_element_type=...  7.56 us
    dot_general x1, matrix products, local(): jnp.einsum('tpgx,tpg->tx', tiles_now, dir_rows, preferred_element_type=jn...  6.55 us
    pallas_call x1, Pallas kernels, unpack(): pl.pallas_call(unpack_kernel, grid=(pl.cdiv(size, ROW_CHUNK),), in_specs=...  6.34 us
  transfers between devices with their start and end apart: 4, of which 3 were waited for; matrix products, arithmetic and copies ran while one was open for 16% of the time, Pallas kernels for 0%

profile of v9, /device:TPU:1, one launch (start us, length us, event | category | flops | bytes accessed | tf_op | source)
XLA Modules:
  0.0 121.3 jit_solution(2709857670373491873)
XLA Ops:
  0.6 0.0 copy-start
  0.6 0.0 copy-start.2
  0.7 0.8 compare_and_fusion
  1.5 0.7 fusion.15
  2.8 0.7 fusion.13
  3.5 0.1 copy.12
  3.6 0.7 fusion.9.w_ref
  4.3 0.0 copy-start.4
  4.3 0.0 copy-start.3
  4.3 17.1 %shard_map.85 = f32[2,1776,128]{2,1,0:T(8,128)S(1)} custom-call(f32[4,2]{1,0:T(4,128)S(1)} %fusion.9.w_ref, bf16[4,59,128,256]{3,2,1,0:T(8,128)(2,1)} %bitcast.54), custom_call_target="tpu_custom_call" | custom-call | tf_op jit(solution)/shard_map/pallas_call | solution.py:103
  21.4 0.0 copy-start.1
  21.4 1.2 %copy-done.1 = f32[2,1776,128]{2,1,0:T(8,128)} copy-done((f32[2,1776,128]{2,1,0:T(8,128)}, f32[2,1776,128]{2,1,0:T(8,128)S(1)}, u32[]{:S(2)}) %copy-start.1) | copy-done | bytes 1818648
  22.6 0.0 copy-done.2
  22.6 0.7 gather_fusion.1
  23.3 0.1 select_bitcast_fusion
  23.4 6.5 %fusion.2 = f32[4,1,256,1]{2,1,3,0:T(1,128)S(1)} fusion(bf16[4,59,128,256]{3,2,1,0:T(8,128)(2,1)} %bitcast.55, bf16[4,59,128,1]{2,0,1,3:T(4,128)(2,1)S(1)} %select_bitcast_fusion), kind=kOutput, calls=%fused_computation.9 | convolution fusion | flops 15466496 | bytes 15531008 | tf_op jit(solution)/shard_map/tpgx,tpg->tx/dot_general | solution.py:188
  29.9 0.1 bitcast_multiply_fusion
  30.0 0.7 broadcast_in_dim.56
  30.7 9.4 %all-to-all-start = ((f32[32,4,257]{2,1,0:T(4,128)}), f32[32,4,257]{2,1,0:T(4,128)S(1)}, u32[]{:S(2)}, u32[]{:S(2)}) async-start(f32[32,4,257]{2,1,0:T(4,128)} %broadcast_in_dim.56), calls=%async_computation | async-start | bytes 393216 | tf_op jit(solution)/shard_map/all_to_all | solution.py:26
  40.1 0.0 copy-done.4
  40.2 0.0 copy-done.3
  40.2 0.0 copy-done
  40.2 0.6 gather_fusion
  40.8 0.1 select_bitcast_fusion.1
  40.9 7.6 %fusion.6 = f32[4,1,59,128]{3,1,2,0:T(1,128)S(1)} fusion(bf16[4,59,128,256]{3,2,1,0:T(8,128)(2,1)} %bitcast.56, bf16[4,256,1,1]{1,0,2,3:T(4,128)(2,1)S(1)} %select_bitcast_fusion.1), kind=kOutput, calls=%fused_computation.22 | convolution fusion | flops 15466496 | bytes 15589376 | tf_op jit(solution)/shard_map/tpgx,tx->tpg/dot_general | solution.py:200
  48.5 0.0 all-to-all-done
  48.5 4.4 %all-to-all-start.2 = ((f32[4,888,128]{2,1,0:T(8,128)}), f32[4,888,128]{2,1,0:T(8,128)}, u32[]{:S(2)}, u32[]{:S(2)}) async-start(f32[4,888,128]{2,1,0:T(8,128)} %bitcast.53), calls=%async_computation.2 | async-start | bytes 3637248 | tf_op jit(solution)/shard_map/all_to_all | solution.py:182
  52.9 0.1 reshape.159
  53.0 0.1 slice_reduce_fusion
  53.1 0.2 fusion
  53.3 7.6 %fusion.4 = f32[4,1,59,128]{3,1,2,0:T(1,128)S(1)} fusion(bf16[4,59,128,256]{3,2,1,0:T(8,128)(2,1)} %bitcast.57, bf16[4,256,1,1]{1,0,2,3:T(4,128)(2,1)S(1)} %fusion), kind=kOutput, calls=%fused_computation.20 | convolution fusion | flops 15466496 | bytes 15589376 | tf_op jit(solution)/shard_map/tpgx,tx->tpg/dot_general | solution.py:197
  60.9 0.4 multiply_reduce_fusion.1
  61.3 0.1 copy.13
  61.4 14.6 %all-to-all-done.2 = f32[4,888,128]{2,1,0:T(8,128)} async-done(((f32[4,888,128]{2,1,0:T(8,128)}), f32[4,888,128]{2,1,0:T(8,128)}, u32[]{:S(2)}, u32[]{:S(2)}) %all-to-all-start.2) | async-done | bytes 1818656 | tf_op jit(solution)/shard_map/all_to_all | solution.py:182
  76.1 0.9 broadcast_in_dim.57
  77.0 3.5 %all-to-all-start.1 = ((f32[4,2,2,59,128]{4,2,3,1,0:T(2,128)}), f32[4,2,2,59,128]{4,2,3,1,0:T(2,128)S(1)}, u32[]{:S(2)}, u32[]{:S(2)}) async-start(f32[4,2,2,59,128]{4,2,3,1,0:T(2,128)} %broadcast_in_dim.57), calls=%async_computation.1 | async-start | bytes 966656 | tf_op jit(solution)/shard_map/all_to_all | solution.py:26
  80.5 1.7 %reduce_sum.39 = f32[888,128]{1,0:T(8,128)S(1)} reduce(f32[4,888,128]{2,1,0:T(8,128)} %all-to-all-done.2, f32[]{:T(128)} %constant.32.clone.1), dimensions={0}, to_apply=%region_3.4 | reduce | flops 340992 | bytes 2273284 | tf_op jit(solution)/shard_map/reduce_sum | solution.py:182
  82.1 5.9 %all-to-all-done.1 = f32[4,2,2,59,128]{4,2,3,1,0:T(2,128)S(1)} async-done(((f32[4,2,2,59,128]{4,2,3,1,0:T(2,128)}), f32[4,2,2,59,128]{4,2,3,1,0:T(2,128)S(1)}, u32[]{:S(2)}, u32[]{:S(2)}) %all-to-all-start.1) | async-done | bytes 483360 | tf_op jit(solution)/shard_map/all_to_all | solution.py:26
  88.1 1.3 %broadcast_in_dim.58 = f32[4,888,128]{2,1,0:T(8,128)} broadcast(f32[888,128]{1,0:T(8,128)S(1)} %reduce_sum.39), dimensions={1,2} | broadcast | bytes 2273280 | tf_op jit(solution)/shard_map/broadcast_in_dim | solution.py:27
  89.4 4.6 %all-to-all-start.3 = ((f32[4,888,128]{2,1,0:T(8,128)}), f32[4,888,128]{2,1,0:T(8,128)}, u32[]{:S(2)}, u32[]{:S(2)}) async-start(f32[4,888,128]{2,1,0:T(8,128)} %broadcast_in_dim.58), calls=%async_computation.3 | async-start | bytes 3637248 | tf_op jit(solution)/shard_map/all_to_all | solution.py:26
  94.0 0.2 reduce_sum.38
  94.2 0.7 slice_bitcast_fusion
  94.9 20.1 %all-to-all-done.3 = f32[4,888,128]{2,1,0:T(8,128)} async-done(((f32[4,888,128]{2,1,0:T(8,128)}), f32[4,888,128]{2,1,0:T(8,128)}, u32[]{:S(2)}, u32[]{:S(2)}) %all-to-all-start.3) | async-done | bytes 1818656 | tf_op jit(solution)/shard_map/all_to_all | solution.py:26
  115.0 6.3 %shard_map.86 = f32[59,59,2,128]{3,2,1,0:T(2,128)} custom-call(f32[2,1776,128]{2,1,0:T(8,128)} %bitcast.20.packed_ref), custom_call_target="tpu_custom_call" | custom-call | tf_op jit(solution)/shard_map/pallas_call | solution.py:154
  (10 shorter events, 0.1 us)
Async XLA Ops:
  0.6 39.6 %copy-start = (bf16[1,4096,256]{2,1,0:T(8,128)(2,1)S(1)}, bf16[1,4096,256]{2,1,0:T(8,128)(2,1)}, u32[]{:S(2)}) copy-start(bf16[1,4096,256]{2,1,0:T(8,128)(2,1)} %param.10) | copy-start | bytes 6291460
  0.6 22.0 %copy-start.2 = (bf16[2,59,128]{2,0,1:T(2,128)(2,1)S(1)}, bf16[2,59,128]{2,0,1:T(2,128)(2,1)}, u32[]{:S(2)}) copy-start(bf16[2,59,128]{2,0,1:T(2,128)(2,1)} %param.11) | copy-start | bytes 90628
  4.3 35.9 %copy-start.4 = (s32[1,4]{1,0:T(1,128)S(1)}, s32[1,4]{1,0:T(1,128)}, u32[]{:S(2)}) copy-start(s32[1,4]{1,0:T(1,128)} %param.9) | copy-start | bytes 52
  4.3 35.9 %copy-start.3 = (s32[1,4]{1,0:T(1,128)S(1)}, s32[1,4]{1,0:T(1,128)}, u32[]{:S(2)}) copy-start(s32[1,4]{1,0:T(1,128)} %param.8) | copy-start | bytes 52
  21.4 1.2 %copy-start.1 = (f32[2,1776,128]{2,1,0:T(8,128)}, f32[2,1776,128]{2,1,0:T(8,128)S(1)}, u32[]{:S(2)}) copy-start(f32[2,1776,128]{2,1,0:T(8,128)S(1)} %shard_map.85) | copy-start | bytes 5455876
  30.7 17.8 %all-to-all-start = ((f32[32,4,257]{2,1,0:T(4,128)}), f32[32,4,257]{2,1,0:T(4,128)S(1)}, u32[]{:S(2)}, u32[]{:S(2)}) async-start(f32[32,4,257]{2,1,0:T(4,128)} %broadcast_in_dim.56), calls=%async_computation | async-start | bytes 393216 | tf_op jit(solution)/shard_map/all_to_all | solution.py:26
  48.5 27.6 %all-to-all-start.2 = ((f32[4,888,128]{2,1,0:T(8,128)}), f32[4,888,128]{2,1,0:T(8,128)}, u32[]{:S(2)}, u32[]{:S(2)}) async-start(f32[4,888,128]{2,1,0:T(8,128)} %bitcast.53), calls=%async_computation.2 | async-start | bytes 3637248 | tf_op jit(solution)/shard_map/all_to_all | solution.py:182
  77.0 11.1 %all-to-all-start.1 = ((f32[4,2,2,59,128]{4,2,3,1,0:T(2,128)}), f32[4,2,2,59,128]{4,2,3,1,0:T(2,128)S(1)}, u32[]{:S(2)}, u32[]{:S(2)}) async-start(f32[4,2,2,59,128]{4,2,3,1,0:T(2,128)} %broadcast_in_dim.57), calls=%async_computation.1 | async-start | bytes 966656 | tf_op jit(solution)/shard_map/all_to_all | solution.py:26
  89.4 25.6 %all-to-all-start.3 = ((f32[4,888,128]{2,1,0:T(8,128)}), f32[4,888,128]{2,1,0:T(8,128)}, u32[]{:S(2)}, u32[]{:S(2)}) async-start(f32[4,888,128]{2,1,0:T(8,128)} %broadcast_in_dim.58), calls=%async_computation.3 | async-start | bytes 3637248 | tf_op jit(solution)/shard_map/all_to_all | solution.py:26

commit v10 on v8

--- a/solution.py
+++ b/solution.py
@@ -34,7 +34,7 @@
 
 
 P_PAD = 64
-GROUP = 4
+GROUP = 2
 
 
 def row_offsets(size):
@@ -78,13 +78,16 @@
                 sc_ref[pl.ds(r * gb * 8 + g * 8, 8), :] = block[r * 8:(r + 1) * 8]
 
     odd = (lax.broadcasted_iota(jnp.int32, (P_PAD, gb), 1) % 2) == 1
-    weights = [w_ref[t, b] for b in range(nb)]
+    alive = w_ref[t, 0]
+    blk = jnp.int32(0)
+    for b in range(1, nb):
+        alive = alive + w_ref[t, b]
+        blk = jnp.where(w_ref[t, b] > 0, jnp.int32(b), blk)
     for p in range(size):
         s = sc_ref[pl.ds((p // 8) * gb * 8 + p % 8, gb, stride=8), :]
         tr = s.T
         row = jnp.where(odd, tr[P_PAD:2 * P_PAD], tr[0:P_PAD])
-        for b in range(nb):
-            acc_ref[b, p] += weights[b] * row
+        acc_ref[blk, p] += alive * row
 
     @pl.when(t == pl.num_programs(0) - 1)
     def _pack():

time: 103 us -> 103 us (level)
  transfers between devices with their start and end apart: 2 -> 2, of which waited for: 1 -> 1; matrix products, arithmetic and copies ran while one was open for 25% -> 26% of each run, Pallas kernels for 0% -> 0%
where the time goes in v10:
time: 103 us
  Pallas kernels  23.3 us (23%)
  matrix products  22.2 us (22%)
  blocking collectives  17.8 us (17%)
  between operations  15 us (15%)
  starting transfers between devices  9.46 us (9%)
  waiting for transfers between devices  9.13 us (9%)
  local copies, waits for them, and re-layouts  4.41 us (4%)
  other arithmetic  1.65 us (2%)
    all_to_all x1, blocking collectives, copy_for_each(): lax.all_to_all(jnp.broadcast_to(array[None], (length, *array.shape)), axi...  17.8 us
    pallas_call x1, Pallas kernels, gram_packed(): pl.pallas_call(gram_kernel, grid=(nt,), in_specs=[pl.BlockSpec(memory_spa...  16.9 us
    all_to_all x1, starting transfers between devices, copy_for_each(): lax.all_to_all(jnp.broadcast_to(array[None], (length, *array.shape)), axi...  9.42 us
    psum x1, waiting for transfers between devices, local(): summed = lax.psum(packed_gram, 'view')  9.11 us
    dot_general x1, matrix products, local(): jnp.einsum('tpgx,tx->tpg', tiles_now, resid_rows, preferred_element_type=...  7.73 us
    dot_general x1, matrix products, local(): jnp.einsum('tpgx,tx->tpg', tiles_now, jp_round, preferred_element_type=jn...  7.73 us
    dot_general x1, matrix products, local(): jnp.einsum('tpgx,tpg->tx', tiles_now, dir_rows, preferred_element_type=jn...  6.55 us
    pallas_call x1, Pallas kernels, unpack(): pl.pallas_call(unpack_kernel, grid=(pl.cdiv(size, ROW_CHUNK),), in_specs=...  6.34 us
  transfers between devices with their start and end apart: 2, of which 1 were waited for; matrix products, arithmetic and copies ran while one was open for 26% of the time, Pallas kernels for 0%

profile of v10, /device:TPU:1, one launch (start us, length us, event | category | flops | bytes accessed | tf_op | source)
XLA Modules:
  0.0 103.0 jit_solution(6196185556037078921)
XLA Ops:
  7.2 0.0 copy-start
  7.2 0.0 copy-start.3
  7.2 0.0 copy-start.4
  7.2 0.0 copy-start.2
  7.2 0.0 all-reduce.2.cloned.1.call-start
  8.1 0.7 fusion.9.w_ref
  8.8 16.9 %shard_map.85 = f32[2,1770,128]{2,1,0:T(8,128)S(1)} custom-call(f32[4,2]{1,0:T(4,128)S(1)} %fusion.9.w_ref, bf16[4,59,128,256]{3,2,1,0:T(8,128)(2,1)} %bitcast.51), custom_call_target="tpu_custom_call" | custom-call | tf_op jit(solution)/shard_map/pallas_call | solution.py:104
  25.7 0.0 copy-start.1
  25.7 1.2 %copy-done.1 = f32[2,1770,128]{2,1,0:T(8,128)} copy-done((f32[2,1770,128]{2,1,0:T(8,128)}, f32[2,1770,128]{2,1,0:T(8,128)S(1)}, u32[]{:S(2)}) %copy-start.1) | copy-done | bytes 1812504
  27.0 0.0 all-reduce.2.cloned.1.call-update
  27.0 0.0 copy-done.3
  27.0 0.0 copy-done.4
  27.0 0.1 copy.12
  27.1 0.0 copy-done.2
  27.1 0.7 gather_fusion.1
  27.8 0.1 select_bitcast_fusion
  27.9 6.5 %fusion.2 = f32[4,1,256,1]{2,1,3,0:T(1,128)S(1)} fusion(bf16[4,59,128,256]{3,2,1,0:T(8,128)(2,1)} %bitcast.52, bf16[4,59,128,1]{2,0,1,3:T(4,128)(2,1)S(1)} %select_bitcast_fusion), kind=kOutput, calls=%fused_computation.9 | convolution fusion | flops 15466496 | bytes 15531008 | tf_op jit(solution)/shard_map/tpgx,tpg->tx/dot_general | solution.py:186
  34.5 0.1 bitcast_multiply_fusion
  34.5 0.7 broadcast_in_dim.50
  35.3 9.4 %all-to-all-start = ((f32[32,4,257]{2,1,0:T(4,128)}), f32[32,4,257]{2,1,0:T(4,128)S(1)}, u32[]{:S(2)}, u32[]{:S(2)}) async-start(f32[32,4,257]{2,1,0:T(4,128)} %broadcast_in_dim.50), calls=%async_computation | async-start | bytes 393216 | tf_op jit(solution)/shard_map/all_to_all | solution.py:26
  44.7 0.0 copy-done
  44.7 0.6 gather_fusion
  45.3 0.1 select_bitcast_fusion.1
  45.4 7.7 %fusion.6 = f32[4,1,59,128]{3,1,2,0:T(1,128)S(1)} fusion(bf16[4,59,128,256]{3,2,1,0:T(8,128)(2,1)} %bitcast.53, bf16[4,256,1,1]{1,0,2,3:T(4,128)(2,1)S(1)} %select_bitcast_fusion.1), kind=kOutput, calls=%fused_computation.22 | convolution fusion | flops 15466496 | bytes 15589376 | tf_op jit(solution)/shard_map/tpgx,tx->tpg/dot_general | solution.py:198
  53.2 0.0 all-to-all-done
  53.2 0.1 reshape.152
  53.3 0.1 slice_reduce_fusion
  53.4 0.2 fusion
  53.6 7.7 %fusion.4 = f32[4,1,59,128]{3,1,2,0:T(1,128)S(1)} fusion(bf16[4,59,128,256]{3,2,1,0:T(8,128)(2,1)} %bitcast.54, bf16[4,256,1,1]{1,0,2,3:T(4,128)(2,1)S(1)} %fusion), kind=kOutput, calls=%fused_computation.20 | convolution fusion | flops 15466496 | bytes 15589376 | tf_op jit(solution)/shard_map/tpgx,tx->tpg/dot_general | solution.py:195
  61.3 0.4 multiply_reduce_fusion.1
  61.7 0.1 copy.13
  61.8 0.1 broadcast_in_dim.51
  62.0 17.8 %all_to_all.10 = f32[4,2,2,59,128]{4,2,3,1,0:T(2,128)S(1)} all-to-all(f32[4,2,2,59,128]{4,2,3,1,0:T(2,128)S(1)} %broadcast_in_dim.51), channel_id=1, replica_groups=mesh['view'=4,'gauss'=32] {'view'}, dimensions={0} | all-to-all | bytes 966656 | tf_op jit(solution)/shard_map/all_to_all | solution.py:26
  79.8 0.2 reduce_sum.29
  80.0 0.7 slice_bitcast_fusion
  80.7 9.1 %all-reduce.2.cloned.1.call-done.packed_ref = f32[2,1770,128]{2,1,0:T(8,128)} async-done(((f32[2,1770,128]{2,1,0:T(8,128)}), f32[2,1770,128]{2,1,0:T(8,128)}) %all-reduce.2.cloned.1.call-update) | async-done | bytes 1812496 | tf_op jit(solution)/shard_map/psum | solution.py:181
  89.8 6.3 %shard_map.86 = f32[59,59,2,128]{3,2,1,0:T(2,128)} custom-call(f32[2,1770,128]{2,1,0:T(8,128)} %all-reduce.2.cloned.1.call-done.packed_ref), custom_call_target="tpu_custom_call" | custom-call | tf_op jit(solution)/shard_map/pallas_call | solution.py:155
  (13 shorter events, 0.1 us)
Async XLA Ops:
  7.2 37.6 %copy-start = (bf16[1,4096,256]{2,1,0:T(8,128)(2,1)S(1)}, bf16[1,4096,256]{2,1,0:T(8,128)(2,1)}, u32[]{:S(2)}) copy-start(bf16[1,4096,256]{2,1,0:T(8,128)(2,1)} %param.10) | copy-start | bytes 6291460
  7.2 19.8 %copy-start.3 = (s32[1,4]{1,0:T(1,128)S(1)}, s32[1,4]{1,0:T(1,128)}, u32[]{:S(2)}) copy-start(s32[1,4]{1,0:T(1,128)} %param.8) | copy-start | bytes 52
  7.2 19.8 %copy-start.4 = (s32[1,4]{1,0:T(1,128)S(1)}, s32[1,4]{1,0:T(1,128)}, u32[]{:S(2)}) copy-start(s32[1,4]{1,0:T(1,128)} %param.9) | copy-start | bytes 52
  7.2 19.9 %copy-start.2 = (bf16[2,59,128]{2,0,1:T(2,128)(2,1)S(1)}, bf16[2,59,128]{2,0,1:T(2,128)(2,1)}, u32[]{:S(2)}) copy-start(bf16[2,59,128]{2,0,1:T(2,128)(2,1)} %param.11) | copy-start | bytes 90628
  7.2 82.6 %all-reduce.2.cloned.1.call-start = ((), (), s32[]{:S(2)}) async-start(), calls=%async_computation.2 | async-start | bytes 3637248 | tf_op jit(solution)/shard_map/psum | solution.py:181
  25.7 1.2 %copy-start.1 = (f32[2,1770,128]{2,1,0:T(8,128)}, f32[2,1770,128]{2,1,0:T(8,128)S(1)}, u32[]{:S(2)}) copy-start(f32[2,1770,128]{2,1,0:T(8,128)S(1)} %shard_map.85) | copy-start | bytes 5437444
  35.3 17.9 %all-to-all-start = ((f32[32,4,257]{2,1,0:T(4,128)}), f32[32,4,257]{2,1,0:T(4,128)S(1)}, u32[]{:S(2)}, u32[]{:S(2)}) async-start(f32[32,4,257]{2,1,0:T(4,128)} %broadcast_in_dim.50), calls=%async_computation | async-start | bytes 393216 | tf_op jit(solution)/shard_map/all_to_all | solution.py:26
Sparse Core Ops, SparseCore 0:
  27.1 62.6 all-reduce.1

commit v11 on v10

--- a/solution.py
+++ b/solution.py
@@ -119,7 +119,7 @@
     )(weights, tiles)
 
 
-ROW_CHUNK = 8
+ROW_CHUNK = 16
 
 
 def unpack_kernel(packed_ref, out_ref, u_ref):

time: 103 us -> 102 us (level)
  no operation moved by 1% of the time
where the time goes in v11:
time: 102 us
  Pallas kernels  22.3 us (22%)
  matrix products  22.2 us (22%)
  blocking collectives  17.8 us (17%)
  between operations  15 us (15%)
  starting transfers between devices  9.46 us (9%)
  waiting for transfers between devices  9.13 us (9%)
  local copies, waits for them, and re-layouts  4.41 us (4%)
  other arithmetic  1.65 us (2%)
    all_to_all x1, blocking collectives, copy_for_each(): lax.all_to_all(jnp.broadcast_to(array[None], (length, *array.shape)), axi...  17.8 us
    pallas_call x1, Pallas kernels, gram_packed(): pl.pallas_call(gram_kernel, grid=(nt,), in_specs=[pl.BlockSpec(memory_spa...  16.9 us
    all_to_all x1, starting transfers between devices, copy_for_each(): lax.all_to_all(jnp.broadcast_to(array[None], (length, *array.shape)), axi...  9.42 us
    psum x1, waiting for transfers between devices, local(): summed = lax.psum(packed_gram, 'view')  9.11 us
    dot_general x1, matrix products, local(): jnp.einsum('tpgx,tx->tpg', tiles_now, resid_rows, preferred_element_type=...  7.73 us
    dot_general x1, matrix products, local(): jnp.einsum('tpgx,tx->tpg', tiles_now, jp_round, preferred_element_type=jn...  7.73 us
    dot_general x1, matrix products, local(): jnp.einsum('tpgx,tpg->tx', tiles_now, dir_rows, preferred_element_type=jn...  6.55 us
    pallas_call x1, Pallas kernels, unpack(): pl.pallas_call(unpack_kernel, grid=(pl.cdiv(size, ROW_CHUNK),), in_specs=...  5.39 us
  transfers between devices with their start and end apart: 2, of which 1 were waited for; matrix products, arithmetic and copies ran while one was open for 26% of the time, Pallas kernels for 0%

profile of v11, /device:TPU:1, one launch (start us, length us, event | category | flops | bytes accessed | tf_op | source)
XLA Modules:
  0.0 102.0 jit_solution(17178104790643341943)
XLA Ops:
  7.2 0.0 copy-start
  7.2 0.0 copy-start.3
  7.2 0.0 copy-start.4
  7.2 0.0 copy-start.2
  7.2 0.0 all-reduce.2.cloned.1.call-start
  8.1 0.7 fusion.9.w_ref
  8.8 16.9 %shard_map.85 = f32[2,1770,128]{2,1,0:T(8,128)S(1)} custom-call(f32[4,2]{1,0:T(4,128)S(1)} %fusion.9.w_ref, bf16[4,59,128,256]{3,2,1,0:T(8,128)(2,1)} %bitcast.51), custom_call_target="tpu_custom_call" | custom-call | tf_op jit(solution)/shard_map/pallas_call | solution.py:104
  25.7 0.0 copy-start.1
  25.7 1.2 %copy-done.1 = f32[2,1770,128]{2,1,0:T(8,128)} copy-done((f32[2,1770,128]{2,1,0:T(8,128)}, f32[2,1770,128]{2,1,0:T(8,128)S(1)}, u32[]{:S(2)}) %copy-start.1) | copy-done | bytes 1812504
  27.0 0.0 all-reduce.2.cloned.1.call-update
  27.0 0.0 copy-done.3
  27.0 0.0 copy-done.4
  27.0 0.1 copy.12
  27.1 0.0 copy-done.2
  27.1 0.7 gather_fusion.1
  27.8 0.1 select_bitcast_fusion
  27.9 6.5 %fusion.2 = f32[4,1,256,1]{2,1,3,0:T(1,128)S(1)} fusion(bf16[4,59,128,256]{3,2,1,0:T(8,128)(2,1)} %bitcast.52, bf16[4,59,128,1]{2,0,1,3:T(4,128)(2,1)S(1)} %select_bitcast_fusion), kind=kOutput, calls=%fused_computation.9 | convolution fusion | flops 15466496 | bytes 15531008 | tf_op jit(solution)/shard_map/tpgx,tpg->tx/dot_general | solution.py:186
  34.5 0.1 bitcast_multiply_fusion
  34.5 0.7 broadcast_in_dim.50
  35.3 9.4 %all-to-all-start = ((f32[32,4,257]{2,1,0:T(4,128)}), f32[32,4,257]{2,1,0:T(4,128)S(1)}, u32[]{:S(2)}, u32[]{:S(2)}) async-start(f32[32,4,257]{2,1,0:T(4,128)} %broadcast_in_dim.50), calls=%async_computation | async-start | bytes 393216 | tf_op jit(solution)/shard_map/all_to_all | solution.py:26
  44.7 0.0 copy-done
  44.7 0.6 gather_fusion
  45.3 0.1 select_bitcast_fusion.1
  45.4 7.7 %fusion.6 = f32[4,1,59,128]{3,1,2,0:T(1,128)S(1)} fusion(bf16[4,59,128,256]{3,2,1,0:T(8,128)(2,1)} %bitcast.53, bf16[4,256,1,1]{1,0,2,3:T(4,128)(2,1)S(1)} %select_bitcast_fusion.1), kind=kOutput, calls=%fused_computation.22 | convolution fusion | flops 15466496 | bytes 15589376 | tf_op jit(solution)/shard_map/tpgx,tx->tpg/dot_general | solution.py:198
  53.2 0.0 all-to-all-done
  53.2 0.1 reshape.152
  53.3 0.1 slice_reduce_fusion
  53.4 0.2 fusion
  53.6 7.7 %fusion.4 = f32[4,1,59,128]{3,1,2,0:T(1,128)S(1)} fusion(bf16[4,59,128,256]{3,2,1,0:T(8,128)(2,1)} %bitcast.54, bf16[4,256,1,1]{1,0,2,3:T(4,128)(2,1)S(1)} %fusion), kind=kOutput, calls=%fused_computation.20 | convolution fusion | flops 15466496 | bytes 15589376 | tf_op jit(solution)/shard_map/tpgx,tx->tpg/dot_general | solution.py:195
  61.3 0.4 multiply_reduce_fusion.1
  61.7 0.1 copy.13
  61.8 0.1 broadcast_in_dim.51
  62.0 17.8 %all_to_all.10 = f32[4,2,2,59,128]{4,2,3,1,0:T(2,128)S(1)} all-to-all(f32[4,2,2,59,128]{4,2,3,1,0:T(2,128)S(1)} %broadcast_in_dim.51), channel_id=1, replica_groups=mesh['view'=4,'gauss'=32] {'view'}, dimensions={0} | all-to-all | bytes 966656 | tf_op jit(solution)/shard_map/all_to_all | solution.py:26
  79.8 0.2 reduce_sum.29
  80.0 0.7 slice_bitcast_fusion
  80.7 9.1 %all-reduce.2.cloned.1.call-done.packed_ref = f32[2,1770,128]{2,1,0:T(8,128)} async-done(((f32[2,1770,128]{2,1,0:T(8,128)}), f32[2,1770,128]{2,1,0:T(8,128)}) %all-reduce.2.cloned.1.call-update) | async-done | bytes 1812496 | tf_op jit(solution)/shard_map/psum | solution.py:181
  89.8 5.4 %shard_map.86 = f32[59,59,2,128]{3,2,1,0:T(2,128)} custom-call(f32[2,1770,128]{2,1,0:T(8,128)} %all-reduce.2.cloned.1.call-done.packed_ref), custom_call_target="tpu_custom_call" | custom-call | tf_op jit(solution)/shard_map/pallas_call | solution.py:155
  (13 shorter events, 0.1 us)
Async XLA Ops:
  7.2 37.6 %copy-start = (bf16[1,4096,256]{2,1,0:T(8,128)(2,1)S(1)}, bf16[1,4096,256]{2,1,0:T(8,128)(2,1)}, u32[]{:S(2)}) copy-start(bf16[1,4096,256]{2,1,0:T(8,128)(2,1)} %param.10) | copy-start | bytes 6291460
  7.2 19.8 %copy-start.3 = (s32[1,4]{1,0:T(1,128)S(1)}, s32[1,4]{1,0:T(1,128)}, u32[]{:S(2)}) copy-start(s32[1,4]{1,0:T(1,128)} %param.8) | copy-start | bytes 52
  7.2 19.8 %copy-start.4 = (s32[1,4]{1,0:T(1,128)S(1)}, s32[1,4]{1,0:T(1,128)}, u32[]{:S(2)}) copy-start(s32[1,4]{1,0:T(1,128)} %param.9) | copy-start | bytes 52
  7.2 19.9 %copy-start.2 = (bf16[2,59,128]{2,0,1:T(2,128)(2,1)S(1)}, bf16[2,59,128]{2,0,1:T(2,128)(2,1)}, u32[]{:S(2)}) copy-start(bf16[2,59,128]{2,0,1:T(2,128)(2,1)} %param.11) | copy-start | bytes 90628
  7.2 82.6 %all-reduce.2.cloned.1.call-start = ((), (), s32[]{:S(2)}) async-start(), calls=%async_computation.2 | async-start | bytes 3637248 | tf_op jit(solution)/shard_map/psum | solution.py:181
  25.7 1.2 %copy-start.1 = (f32[2,1770,128]{2,1,0:T(8,128)}, f32[2,1770,128]{2,1,0:T(8,128)S(1)}, u32[]{:S(2)}) copy-start(f32[2,1770,128]{2,1,0:T(8,128)S(1)} %shard_map.85) | copy-start | bytes 5437444
  35.3 17.9 %all-to-all-start = ((f32[32,4,257]{2,1,0:T(4,128)}), f32[32,4,257]{2,1,0:T(4,128)S(1)}, u32[]{:S(2)}, u32[]{:S(2)}) async-start(f32[32,4,257]{2,1,0:T(4,128)} %broadcast_in_dim.50), calls=%async_computation | async-start | bytes 393216 | tf_op jit(solution)/shard_map/all_to_all | solution.py:26
Sparse Core Ops, SparseCore 0:
  27.1 62.6 all-reduce.1

commit v12 on v11

--- a/solution.py
+++ b/solution.py
@@ -119,7 +119,7 @@
     )(weights, tiles)
 
 
-ROW_CHUNK = 16
+ROW_CHUNK = 32
 
 
 def unpack_kernel(packed_ref, out_ref, u_ref):

time: 102 us -> 102 us (level)
  no operation moved by 1% of the time
where the time goes in v12:
time: 102 us
  Pallas kernels  22.4 us (22%)
  matrix products  22.2 us (22%)
  blocking collectives  17.8 us (17%)
  between operations  15 us (15%)
  starting transfers between devices  9.46 us (9%)
  waiting for transfers between devices  9.13 us (9%)
  local copies, waits for them, and re-layouts  4.41 us (4%)
  other arithmetic  1.65 us (2%)
    all_to_all x1, blocking collectives, copy_for_each(): lax.all_to_all(jnp.broadcast_to(array[None], (length, *array.shape)), axi...  17.8 us
    pallas_call x1, Pallas kernels, gram_packed(): pl.pallas_call(gram_kernel, grid=(nt,), in_specs=[pl.BlockSpec(memory_spa...  16.9 us
    all_to_all x1, starting transfers between devices, copy_for_each(): lax.all_to_all(jnp.broadcast_to(array[None], (length, *array.shape)), axi...  9.42 us
    psum x1, waiting for transfers between devices, local(): summed = lax.psum(packed_gram, 'view')  9.11 us
    dot_general x1, matrix products, local(): jnp.einsum('tpgx,tx->tpg', tiles_now, resid_rows, preferred_element_type=...  7.73 us
    dot_general x1, matrix products, local(): jnp.einsum('tpgx,tx->tpg', tiles_now, jp_round, preferred_element_type=jn...  7.73 us
    dot_general x1, matrix products, local(): jnp.einsum('tpgx,tpg->tx', tiles_now, dir_rows, preferred_element_type=jn...  6.55 us
    pallas_call x1, Pallas kernels, unpack(): pl.pallas_call(unpack_kernel, grid=(pl.cdiv(size, ROW_CHUNK),), in_specs=...  5.51 us
  transfers between devices with their start and end apart: 2, of which 1 were waited for; matrix products, arithmetic and copies ran while one was open for 26% of the time, Pallas kernels for 0%

profile of v12, /device:TPU:1, one launch (start us, length us, event | category | flops | bytes accessed | tf_op | source)
XLA Modules:
  0.0 102.2 jit_solution(15681559884611931785)
XLA Ops:
  7.2 0.0 copy-start
  7.2 0.0 copy-start.3
  7.2 0.0 copy-start.4
  7.2 0.0 copy-start.2
  7.2 0.0 all-reduce.2.cloned.1.call-start
  8.1 0.7 fusion.9.w_ref
  8.8 16.9 %shard_map.85 = f32[2,1770,128]{2,1,0:T(8,128)S(1)} custom-call(f32[4,2]{1,0:T(4,128)S(1)} %fusion.9.w_ref, bf16[4,59,128,256]{3,2,1,0:T(8,128)(2,1)} %bitcast.51), custom_call_target="tpu_custom_call" | custom-call | tf_op jit(solution)/shard_map/pallas_call | solution.py:104
  25.7 0.0 copy-start.1
  25.7 1.2 %copy-done.1 = f32[2,1770,128]{2,1,0:T(8,128)} copy-done((f32[2,1770,128]{2,1,0:T(8,128)}, f32[2,1770,128]{2,1,0:T(8,128)S(1)}, u32[]{:S(2)}) %copy-start.1) | copy-done | bytes 1812504
  27.0 0.0 all-reduce.2.cloned.1.call-update
  27.0 0.0 copy-done.3
  27.0 0.0 copy-done.4
  27.0 0.1 copy.12
  27.1 0.0 copy-done.2
  27.1 0.7 gather_fusion.1
  27.8 0.1 select_bitcast_fusion
  27.9 6.5 %fusion.2 = f32[4,1,256,1]{2,1,3,0:T(1,128)S(1)} fusion(bf16[4,59,128,256]{3,2,1,0:T(8,128)(2,1)} %bitcast.52, bf16[4,59,128,1]{2,0,1,3:T(4,128)(2,1)S(1)} %select_bitcast_fusion), kind=kOutput, calls=%fused_computation.9 | convolution fusion | flops 15466496 | bytes 15531008 | tf_op jit(solution)/shard_map/tpgx,tpg->tx/dot_general | solution.py:186
  34.5 0.1 bitcast_multiply_fusion
  34.5 0.7 broadcast_in_dim.50
  35.3 9.4 %all-to-all-start = ((f32[32,4,257]{2,1,0:T(4,128)}), f32[32,4,257]{2,1,0:T(4,128)S(1)}, u32[]{:S(2)}, u32[]{:S(2)}) async-start(f32[32,4,257]{2,1,0:T(4,128)} %broadcast_in_dim.50), calls=%async_computation | async-start | bytes 393216 | tf_op jit(solution)/shard_map/all_to_all | solution.py:26
  44.7 0.0 copy-done
  44.7 0.6 gather_fusion
  45.3 0.1 select_bitcast_fusion.1
  45.4 7.7 %fusion.6 = f32[4,1,59,128]{3,1,2,0:T(1,128)S(1)} fusion(bf16[4,59,128,256]{3,2,1,0:T(8,128)(2,1)} %bitcast.53, bf16[4,256,1,1]{1,0,2,3:T(4,128)(2,1)S(1)} %select_bitcast_fusion.1), kind=kOutput, calls=%fused_computation.22 | convolution fusion | flops 15466496 | bytes 15589376 | tf_op jit(solution)/shard_map/tpgx,tx->tpg/dot_general | solution.py:198
  53.2 0.0 all-to-all-done
  53.2 0.1 reshape.152
  53.3 0.1 slice_reduce_fusion
  53.4 0.2 fusion
  53.6 7.7 %fusion.4 = f32[4,1,59,128]{3,1,2,0:T(1,128)S(1)} fusion(bf16[4,59,128,256]{3,2,1,0:T(8,128)(2,1)} %bitcast.54, bf16[4,256,1,1]{1,0,2,3:T(4,128)(2,1)S(1)} %fusion), kind=kOutput, calls=%fused_computation.20 | convolution fusion | flops 15466496 | bytes 15589376 | tf_op jit(solution)/shard_map/tpgx,tx->tpg/dot_general | solution.py:195
  61.3 0.4 multiply_reduce_fusion.1
  61.7 0.1 copy.13
  61.8 0.1 broadcast_in_dim.51
  62.0 17.8 %all_to_all.10 = f32[4,2,2,59,128]{4,2,3,1,0:T(2,128)S(1)} all-to-all(f32[4,2,2,59,128]{4,2,3,1,0:T(2,128)S(1)} %broadcast_in_dim.51), channel_id=1, replica_groups=mesh['view'=4,'gauss'=32] {'view'}, dimensions={0} | all-to-all | bytes 966656 | tf_op jit(solution)/shard_map/all_to_all | solution.py:26
  79.8 0.2 reduce_sum.29
  80.0 0.7 slice_bitcast_fusion
  80.7 9.1 %all-reduce.2.cloned.1.call-done.packed_ref = f32[2,1770,128]{2,1,0:T(8,128)} async-done(((f32[2,1770,128]{2,1,0:T(8,128)}), f32[2,1770,128]{2,1,0:T(8,128)}) %all-reduce.2.cloned.1.call-update) | async-done | bytes 1812496 | tf_op jit(solution)/shard_map/psum | solution.py:181
  89.8 5.5 %shard_map.86 = f32[59,59,2,128]{3,2,1,0:T(2,128)} custom-call(f32[2,1770,128]{2,1,0:T(8,128)} %all-reduce.2.cloned.1.call-done.packed_ref), custom_call_target="tpu_custom_call" | custom-call | tf_op jit(solution)/shard_map/pallas_call | solution.py:155
  (13 shorter events, 0.1 us)
Async XLA Ops:
  7.2 37.6 %copy-start = (bf16[1,4096,256]{2,1,0:T(8,128)(2,1)S(1)}, bf16[1,4096,256]{2,1,0:T(8,128)(2,1)}, u32[]{:S(2)}) copy-start(bf16[1,4096,256]{2,1,0:T(8,128)(2,1)} %param.10) | copy-start | bytes 6291460
  7.2 19.8 %copy-start.3 = (s32[1,4]{1,0:T(1,128)S(1)}, s32[1,4]{1,0:T(1,128)}, u32[]{:S(2)}) copy-start(s32[1,4]{1,0:T(1,128)} %param.8) | copy-start | bytes 52
  7.2 19.8 %copy-start.4 = (s32[1,4]{1,0:T(1,128)S(1)}, s32[1,4]{1,0:T(1,128)}, u32[]{:S(2)}) copy-start(s32[1,4]{1,0:T(1,128)} %param.9) | copy-start | bytes 52
  7.2 19.9 %copy-start.2 = (bf16[2,59,128]{2,0,1:T(2,128)(2,1)S(1)}, bf16[2,59,128]{2,0,1:T(2,128)(2,1)}, u32[]{:S(2)}) copy-start(bf16[2,59,128]{2,0,1:T(2,128)(2,1)} %param.11) | copy-start | bytes 90628
  7.2 82.6 %all-reduce.2.cloned.1.call-start = ((), (), s32[]{:S(2)}) async-start(), calls=%async_computation.2 | async-start | bytes 3637248 | tf_op jit(solution)/shard_map/psum | solution.py:181
  25.7 1.2 %copy-start.1 = (f32[2,1770,128]{2,1,0:T(8,128)}, f32[2,1770,128]{2,1,0:T(8,128)S(1)}, u32[]{:S(2)}) copy-start(f32[2,1770,128]{2,1,0:T(8,128)S(1)} %shard_map.85) | copy-start | bytes 5437444
  35.3 17.9 %all-to-all-start = ((f32[32,4,257]{2,1,0:T(4,128)}), f32[32,4,257]{2,1,0:T(4,128)S(1)}, u32[]{:S(2)}, u32[]{:S(2)}) async-start(f32[32,4,257]{2,1,0:T(4,128)} %broadcast_in_dim.50), calls=%async_computation | async-start | bytes 393216 | tf_op jit(solution)/shard_map/all_to_all | solution.py:26
Sparse Core Ops, SparseCore 0:
  27.1 62.6 all-reduce.1
